TPU v7x, 256 devices: a whole 4x4x8 slice. The times are simulated.
256 devices in a mesh: depth: 8 (over y_hi, x), shots: 32 (over z, y_lo, core).
Axes of the slice: x: 4, y: 4 (y_hi: 2, y_lo: 2; y = y_hi * 2 + y_lo), z: 8, core: 2. Of those that a mesh axis runs over, the one named last changes fastest.
Arguments:
- adj_now: float32 [32, 128, 128, 128], P('shots', 'depth'), may hold values from -6 to 6
- adj_prev: float32 [32, 128, 128, 128], P('shots', 'depth'), may hold values from -6 to 6
- fwd_snap: bfloat16 [32, 4, 128, 128, 128], P('shots', None, 'depth'), may hold values from -6 to 6
- velocity: float32 [128, 128, 128], P('depth', 'shots'), may hold values from 1 to 2
- density: float32 [128, 128, 128], P('depth', 'shots'), may hold values from 1 to 2
- shot_count: int32 [32], P('shots'), may hold values from 1 to 12, 128 in all
- rec_x: int32 [32, 256], P('shots'), may hold values from 0 to 127
- rec_y: int32 [32, 256], P('shots'), may hold values from 0 to 127
- residual: float32 [32, 4, 256], P('shots'), may hold values from -6 to 6
Outputs:
- out_now: float32 [32, 128, 128, 128], P('shots', 'depth')
- out_prev: float32 [32, 128, 128, 128], P('shots', 'depth')
- grad_vel: float32 [128, 128, 128], P('depth', 'shots')
Inputs may be any that keep to these rules, and one draw needn't show every extreme that they name: `shot_count`: the counts sum to 128; the largest is exactly 12.
All inputs are finite; a program needn't handle non-finite values.
Results may differ from a plain program's by a relative error of at most 0.0003.
Values sent between devices are 32-bit elements; how exact they have to be, the bound alone decides.
No kernel may reach another device: no remote copies, remote signals or barrier semaphores. Data moves between devices by JAX's collectives and lax.ppermute only.
A program may use at most 64 MiB of HBM per device.

v0:
```python
import jax
import jax.numpy as jnp
from jax import lax
from jax.sharding import PartitionSpec as P


def with_halo(shard, sides, width):
    for axis, dim in sides:
        peers, length = (lax.axis_size(axis), shard.shape[dim])
        up = [(i, (i + 1) % peers) for i in range(peers - 1)]
        down = [(j, i) for i, j in up]
        last = lax.slice_in_dim(shard, length - width, length, axis=dim)
        first = lax.slice_in_dim(shard, 0, width, axis=dim)
        before = lax.ppermute(last, axis, up)
        after = lax.ppermute(first, axis, down)
        shard = jnp.concatenate([before, shard, after], axis=dim)
    return shard


def operate(field, buoy):
    padded = jnp.pad(field, 1)
    bpad = jnp.pad(buoy, 1)
    total = jnp.zeros_like(field)
    for axis in range(3):
        center = [slice(1, -1)] * 3
        ahead = list(center)
        behind = list(center)
        ahead[axis] = slice(2, None)
        behind[axis] = slice(0, -2)
        pc, pa, pb = (padded[tuple(center)], padded[tuple(ahead)], padded[tuple(behind)])
        bc, ba, bb = (bpad[tuple(center)], bpad[tuple(ahead)], bpad[tuple(behind)])
        total = total + 0.5 * (bc + ba) * (pa - pc) - 0.5 * (bb + bc) * (pc - pb)
    return total


def source_plane(rows_x, rows_y, amounts, width_x, width_y):
    onehot_x = (rows_x[:, None] == jnp.arange(width_x, dtype=jnp.int32)[None, :]).astype(
        jnp.float32
    )
    onehot_y = (rows_y[:, None] == jnp.arange(width_y, dtype=jnp.int32)[None, :]).astype(
        jnp.float32
    )
    return jnp.dot((onehot_x * amounts[:, None]).T, onehot_y, precision=lax.Precision.HIGHEST)


def body(adj_now, adj_prev, fwd_snap, velocity, density, shot_count, rec_x, rec_y, residual):
    depth_planes = adj_now.shape[1]
    width_x = adj_now.shape[2]
    width_y = adj_now.shape[3]
    steps = fwd_snap.shape[1]
    groups = lax.axis_size("shots")
    width = 1
    vel_all, rho_all = (
        lax.all_gather(velocity, "shots", axis=1, tiled=True),
        lax.all_gather(density, "shots", axis=1, tiled=True),
    )
    packed = jnp.stack([rho_all * vel_all * vel_all, 1.0 / rho_all])
    extended = with_halo(packed, (("depth", 1),), width)
    buoy_ext = extended[1]
    first = lax.axis_index("depth") * depth_planes
    snaps = fwd_snap[0]
    rows_x = rec_x[0]
    rows_y = rec_y[0]
    image = jnp.zeros((depth_planes, width_x, width_y), jnp.float32)
    kappa_ext = extended[0, width : width + depth_planes]
    global_plane = first + jnp.arange(depth_planes, dtype=jnp.int32)
    at_receivers = (global_plane == 2).astype(jnp.float32)[:, None, None]
    current = adj_now[0]
    older = adj_prev[0]
    for step in range(steps):
        moment = steps - 1 - step
        rimmed_field = with_halo(current[None], (("depth", 1),), 1)[0]
        plane = source_plane(rows_x, rows_y, residual[0, moment], width_x, width_y)
        spread = operate(rimmed_field, buoy_ext)[1:-1]
        newer = (
            2.0 * current - older + 0.08 * kappa_ext * spread + 0.08 * at_receivers * plane[None]
        )
        image = image + snaps[moment].astype(jnp.float32) * newer
        older = current
        current = newer
    weighted = shot_count[0].astype(jnp.float32) * image
    summed = lax.psum_scatter(weighted, "shots", scatter_dimension=1, tiled=True)
    grad_vel = 2.0 * density * velocity * summed / (4.0 * groups)
    return (current[None], older[None], grad_vel)


def solution(mesh):
    in_specs = (
        P("shots", "depth", None, None),
        P("shots", "depth", None, None),
        P("shots", None, "depth", None, None),
        P("depth", "shots", None),
        P("depth", "shots", None),
        P("shots"),
        P("shots", None),
        P("shots", None),
        P("shots", None, None),
    )
    out_specs = (
        P("shots", "depth", None, None),
        P("shots", "depth", None, None),
        P("depth", "shots", None),
    )
    return jax.shard_map(body, mesh=mesh, in_specs=in_specs, out_specs=out_specs, check_vma=False)
```

profile of v0, /device:TPU:24, one launch (start us, length us, event | category | flops | bytes accessed | tf_op | source)
XLA Modules:
  0.0 383.3 jit_solution(11470372513918090008)
XLA Ops:
  7.2 0.0 all-gather.5.cloned.1.call-start
  7.2 1.4 copy.15
  8.6 0.0 all-gather.5.cloned.1.call-update
  8.6 0.0 all-gather.3.cloned.1.call-start
  8.7 1.4 copy.14
  10.1 0.0 all-gather.3.cloned.1.call-update
  10.1 0.0 reduce-scatter.2.cloned.1.call-start
  10.1 0.9 fusion.106
  11.0 5.3 %collective-permute-start.3 = (f32[1,1,128,128]{3,1,2,0:T(1,128)S(1)}, f32[1,1,128,128]{3,1,2,0:T(1,128)S(1)}, u32[]{:S(2)}, u32[]{:S(2)}) collective-permute-start(f32[1,1,128,128]{3,1,2,0:T(1,128)S(1)} %bitcast.68), channel_id=1, source_target_pairs={{32,0},{64,32},{96,64},{128,96},{160,128},{192,160},{224,192},{33,... | collective-permute-start | bytes 196616 | tf_op jit(solution)/shard_map/ppermute | solution.py:15
  16.4 1.9 collective-permute-start.2
  18.3 1.8 copy.12
  20.2 0.4 fusion.79
  20.6 2.9 fusion.102
  23.5 2.6 collective-permute-done.2
  26.2 0.2 maximum_bitcast_fusion
  26.4 49.7 %all-gather.5.cloned.1.call-done = f32[16,128,128]{2,0,1:T(8,128)} async-done(((f32[16,4,128]{2,0,1:T(8,128)}), f32[16,128,128]{2,0,1:T(8,128)}) %all-gather.5.cloned.1.call-update) | async-done | bytes 1048592 | tf_op jit(solution)/shard_map/all_gather | solution.py:54
  76.1 65.7 %all-gather.3.cloned.1.call-done = f32[16,128,128]{2,0,1:T(8,128)} async-done(((f32[16,4,128]{2,0,1:T(8,128)}), f32[16,128,128]{2,0,1:T(8,128)}) %all-gather.3.cloned.1.call-update) | async-done | bytes 1048592 | tf_op jit(solution)/shard_map/all_gather | solution.py:55
  141.8 1.7 multiply_multiply_fusion
  143.6 0.2 pad_maximum_fusion.4
  143.8 5.4 %collective-permute-start.1 = (f32[2,1,128,128]{3,1,2,0:T(1,128)S(1)}, f32[2,1,128,128]{3,1,2,0:T(1,128)S(1)}, u32[]{:S(2)}, u32[]{:S(2)}) collective-permute-start(f32[2,1,128,128]{3,1,2,0:T(1,128)S(1)} %get-tuple-element.13), channel_id=1, source_target_pairs={{32,0},{64,32},{96,64},{128,96},{160,128},{192,160},{224,192},{33,... | collective-permute-start | bytes 393224 | tf_op jit(solution)/shard_map/ppermute | solution.py:15
  149.2 1.9 collective-permute-start
  151.1 4.5 %fusion.12 = (f32[18,128,128]{2,0,1:T(8,128)}, f32[18,128,128]{2,0,1:T(8,128)}, f32[18,128,128]{2,0,1:T(8,128)}, f32[18,128,128]{2,0,1:T(8,128)}, f32[18,128,128]{2,0,1:T(8,128)}, /*index=5*/f32[18,128,128]{2,0,1:T(8,128)}) fusion(f32[18,128,128]{2,0,1:T(8,128)S(1)} %maximum_bitcast_fusion), kind=kLoop, calls=%fused_computation.42 | loop fusion | flops 589824 | bytes 8257536 | tf_op jit(solution)/shard_map/sub | solution.py:32
  155.6 4.4 %collective-permute-done = f32[2,1,128,128]{3,1,2,0:T(1,128)S(1)} collective-permute-done((f32[2,1,128,128]{3,1,2,0:T(1,128)S(1)}, f32[2,1,128,128]{3,1,2,0:T(1,128)S(1)}, u32[]{:S(2)}, u32[]{:S(2)}) %collective-permute-start) | collective-permute-done | bytes 131104 | tf_op jit(solution)/shard_map/ppermute | solution.py:14
  160.0 0.2 fusion.20
  160.3 1.3 fusion.1
  161.6 0.1 copy-done.13
  161.7 0.6 copy-done.4
  162.3 0.3 copy-done.5
  162.6 1.5 copy-done.6
  164.1 0.6 copy-done.7
  164.7 0.4 copy-done.8
  165.1 0.4 copy-done.9
  165.6 0.4 copy-done.10
  166.0 4.0 %fusion.61 = f32[16,128,128]{2,0,1:T(8,128)S(1)} fusion(f32[18,128,128]{2,0,1:T(8,128)S(1)} %copy-done.9, f32[18,128,128]{2,0,1:T(8,128)S(1)} %copy-done.8, f32[18,128,128]{2,0,1:T(8,128)S(1)} %copy-done.7, f32[18,128,128]{2,0,1:T(8,128)S(1)} %copy-done.11, f32[18,128,128]{2,0,1:T(8,128)S(1)} %copy-done.4, f32[18,128,128]{2,0,1:T(8,128)S(1)} %copy-done.10, ...), kind=kLoop, calls=%fused_computation.118 | loop fusion | flops 5767168 | bytes 17891392 | tf_op jit(solution)/shard_map/add | solution.py:76
  170.0 0.1 fusion.105
  170.1 3.1 collective-permute-start.5
  173.3 2.7 collective-permute-start.4
  176.0 0.4 fusion.77
  176.4 6.6 %collective-permute-done.4 = f32[1,1,128,128]{3,1,2,0:T(1,128)S(1)} collective-permute-done((f32[1,1,128,128]{3,1,2,0:T(1,128)S(1)}, f32[1,1,128,128]{3,1,2,0:T(1,128)S(1)}, u32[]{:S(2)}, u32[]{:S(2)}) %collective-permute-start.4) | collective-permute-done | bytes 65568 | tf_op jit(solution)/shard_map/ppermute | solution.py:14
  183.0 1.4 maximum_bitcast_fusion.1
  184.4 10.0 %fusion.14 = (f32[18,128,128]{2,0,1:T(8,128)}, f32[18,128,128]{2,0,1:T(8,128)}, f32[18,128,128]{2,0,1:T(8,128)}, f32[18,128,128]{2,0,1:T(8,128)}, f32[18,128,128]{2,0,1:T(8,128)}, /*index=5*/f32[18,128,128]{2,0,1:T(8,128)}) fusion(f32[18,128,128]{2,0,1:T(8,128)} %maximum_bitcast_fusion.1), kind=kLoop, calls=%fused_computation.44 | loop fusion | flops 589824 | bytes 8257536 | tf_op jit(solution)/shard_map/sub | solution.py:32
  194.4 6.6 %fusion.49 = f32[16,128,128]{2,0,1:T(8,128)S(1)} fusion(f32[18,128,128]{2,0,1:T(8,128)} %get-tuple-element.29, f32[18,128,128]{2,0,1:T(8,128)} %get-tuple-element.28, f32[18,128,128]{2,0,1:T(8,128)} %get-tuple-element.27, f32[18,128,128]{2,0,1:T(8,128)} %get-tuple-element.31, f32[18,128,128]{2,0,1:T(8,128)} %maximum_bitcast_fusion.1, ...), kind=kLoop, calls=%fused_computation.100 | loop fusion | flops 5767168 | bytes 17891392 | tf_op jit(solution)/shard_map/add | solution.py:76
  201.0 0.1 fusion.104
  201.1 1.9 collective-permute-start.7
  203.1 4.1 %collective-permute-start.6 = (f32[1,1,128,128]{3,1,2,0:T(1,128)S(1)}, f32[1,1,128,128]{3,1,2,0:T(1,128)S(1)}, u32[]{:S(2)}, u32[]{:S(2)}) collective-permute-start(f32[1,1,128,128]{3,1,2,0:T(1,128)S(1)} %get-tuple-element.46), channel_id=1, source_target_pairs={{0,32},{32,64},{64,96},{96,128},{128,160},{160,192},{192,224},{1,3... | collective-permute-start | bytes 196616 | tf_op jit(solution)/shard_map/ppermute | solution.py:14
  207.2 0.4 fusion.75
  207.6 5.2 %collective-permute-done.6 = f32[1,1,128,128]{3,1,2,0:T(1,128)S(1)} collective-permute-done((f32[1,1,128,128]{3,1,2,0:T(1,128)S(1)}, f32[1,1,128,128]{3,1,2,0:T(1,128)S(1)}, u32[]{:S(2)}, u32[]{:S(2)}) %collective-permute-start.6) | collective-permute-done | bytes 65568 | tf_op jit(solution)/shard_map/ppermute | solution.py:14
  212.8 1.4 maximum_bitcast_fusion.2
  214.2 10.0 %fusion.16 = (f32[18,128,128]{2,0,1:T(8,128)}, f32[18,128,128]{2,0,1:T(8,128)}, f32[18,128,128]{2,0,1:T(8,128)}, f32[18,128,128]{2,0,1:T(8,128)}, f32[18,128,128]{2,0,1:T(8,128)}, /*index=5*/f32[18,128,128]{2,0,1:T(8,128)}) fusion(f32[18,128,128]{2,0,1:T(8,128)} %maximum_bitcast_fusion.2), kind=kLoop, calls=%fused_computation.46 | loop fusion | flops 589824 | bytes 8257536 | tf_op jit(solution)/shard_map/sub | solution.py:32
  224.2 6.5 %fusion.37 = f32[16,128,128]{2,0,1:T(8,128)S(1)} fusion(f32[18,128,128]{2,0,1:T(8,128)} %get-tuple-element.23, f32[18,128,128]{2,0,1:T(8,128)} %get-tuple-element.22, f32[18,128,128]{2,0,1:T(8,128)} %get-tuple-element.21, f32[18,128,128]{2,0,1:T(8,128)} %get-tuple-element.25, f32[18,128,128]{2,0,1:T(8,128)} %maximum_bitcast_fusion.2, ...), kind=kLoop, calls=%fused_computation.82 | loop fusion | flops 5767168 | bytes 17891392 | tf_op jit(solution)/shard_map/add | solution.py:76
  230.8 0.1 fusion.103
  230.9 1.9 collective-permute-start.9
  232.8 3.9 %collective-permute-start.8 = (f32[1,1,128,128]{3,1,2,0:T(1,128)S(1)}, f32[1,1,128,128]{3,1,2,0:T(1,128)S(1)}, u32[]{:S(2)}, u32[]{:S(2)}) collective-permute-start(f32[1,1,128,128]{3,1,2,0:T(1,128)S(1)} %get-tuple-element.44), channel_id=1, source_target_pairs={{0,32},{32,64},{64,96},{96,128},{128,160},{160,192},{192,224},{1,3... | collective-permute-start | bytes 196616 | tf_op jit(solution)/shard_map/ppermute | solution.py:14
  236.7 0.4 fusion.73
  237.8 4.8 %collective-permute-done.8 = f32[1,1,128,128]{3,1,2,0:T(1,128)S(1)} collective-permute-done((f32[1,1,128,128]{3,1,2,0:T(1,128)S(1)}, f32[1,1,128,128]{3,1,2,0:T(1,128)S(1)}, u32[]{:S(2)}, u32[]{:S(2)}) %collective-permute-start.8) | collective-permute-done | bytes 65568 | tf_op jit(solution)/shard_map/ppermute | solution.py:14
  242.6 1.4 maximum_bitcast_fusion.3
  244.0 10.0 %fusion.18 = (f32[18,128,128]{2,0,1:T(8,128)}, f32[18,128,128]{2,0,1:T(8,128)}, f32[18,128,128]{2,0,1:T(8,128)}, f32[18,128,128]{2,0,1:T(8,128)}, f32[18,128,128]{2,0,1:T(8,128)}, /*index=5*/f32[18,128,128]{2,0,1:T(8,128)}) fusion(f32[18,128,128]{2,0,1:T(8,128)} %maximum_bitcast_fusion.3), kind=kLoop, calls=%fused_computation.48 | loop fusion | flops 589824 | bytes 8257536 | tf_op jit(solution)/shard_map/sub | solution.py:32
  254.0 9.0 %fusion.70 = (f32[16,128,128]{2,0,1:T(8,128)}, f32[16,128,128]{2,0,1:T(8,128)}) fusion(f32[16,128,128]{2,0,1:T(8,128)S(1)} %fusion.37, f32[16,128,128]{2,0,1:T(8,128)} %copy-done.2, f32[16,128,128]{2,0,1:T(8,128)S(1)} %fusion.61, bf16[1,1,16,128,128]{4,3,2,1,0:T(8,128)(2,1)} %get-tuple-element.11, bf16[1,1,16,128,128]{4,3,2,1,0:T(8,128)(2,1)} %get-tuple-element.9, ...), kind=kLoop, calls=%fused_computation.133 | loop fusion | flops 8912896 | bytes 22085700 | tf_op jit(solution)/shard_map/mul | solution.py:81
  262.9 0.0 reduce-scatter.2.cloned.1.call-update
  263.0 1.3 copy.26
  264.3 1.3 copy.25
  265.6 109.8 %reduce-scatter.2.cloned.1.call-done = f32[16,4,128]{2,0,1:T(8,128)} async-done(((f32[16,128,128]{2,0,1:T(8,128)}), f32[16,4,128]{2,0,1:T(8,128)}) %reduce-scatter.2.cloned.1.call-update) | async-done | bytes 32784 | tf_op jit(solution)/shard_map/reduce_scatter | solution.py:82
  375.4 0.8 multiply_multiply_fusion.1
  376.1 0.6 copy.27
  (37 shorter events, 0.1 us)
Async XLA Ops:
  7.2 13.0 %copy-start.16 = (f32[1,4,256]{2,1,0:T(4,128)S(1)}, f32[1,4,256]{2,1,0:T(4,128)}, u32[]{:S(2)}) copy-start(f32[1,4,256]{2,1,0:T(4,128)} %param.17) | copy-start | bytes 12292
  7.2 13.0 %copy-start.17 = (s32[1,256]{1,0:T(1,128)S(1)}, s32[1,256]{1,0:T(1,128)}, u32[]{:S(2)}) copy-start(s32[1,256]{1,0:T(1,128)} %param.16) | copy-start | bytes 3076
  7.2 13.0 %copy-start.18 = (s32[1,256]{1,0:T(1,128)S(1)}, s32[1,256]{1,0:T(1,128)}, u32[]{:S(2)}) copy-start(s32[1,256]{1,0:T(1,128)} %param.15) | copy-start | bytes 3076
  7.2 68.9 %all-gather.5.cloned.1.call-start = ((), (), s32[]{:S(2)}) async-start(), calls=%async_computation.2 | async-start | bytes 1081344 | tf_op jit(solution)/shard_map/all_gather | solution.py:54
  8.6 133.2 %all-gather.3.cloned.1.call-start = ((), (), s32[]{:S(2)}) async-start(), calls=%async_computation.1 | async-start | bytes 1081344 | tf_op jit(solution)/shard_map/all_gather | solution.py:55
  10.1 365.3 %reduce-scatter.2.cloned.1.call-start = ((), (), s32[]{:S(2)}) async-start(), calls=%async_computation.3 | async-start | bytes 1081344 | tf_op jit(solution)/shard_map/reduce_scatter | solution.py:82
  11.0 12.5 %collective-permute-start.3 = (f32[1,1,128,128]{3,1,2,0:T(1,128)S(1)}, f32[1,1,128,128]{3,1,2,0:T(1,128)S(1)}, u32[]{:S(2)}, u32[]{:S(2)}) collective-permute-start(f32[1,1,128,128]{3,1,2,0:T(1,128)S(1)} %bitcast.68), channel_id=1, source_target_pairs={{32,0},{64,32},{96,64},{128,96},{160,128},{192,160},{224,192},{33,... | collective-permute-start | bytes 196616 | tf_op jit(solution)/shard_map/ppermute | solution.py:15
  16.4 9.8 %collective-permute-start.2 = (f32[1,1,128,128]{3,1,2,0:T(1,128)S(1)}, f32[1,1,128,128]{3,1,2,0:T(1,128)S(1)}, u32[]{:S(2)}, u32[]{:S(2)}) collective-permute-start(f32[1,1,128,128]{3,1,2,0:T(1,128)S(1)} %bitcast.67), channel_id=1, source_target_pairs={{0,32},{32,64},{64,96},{96,128},{128,160},{160,192},{192,224},{1,3... | collective-permute-start | bytes 196616 | tf_op jit(solution)/shard_map/ppermute | solution.py:14
  26.4 124.7 %copy-start.3 = (f32[18,128,128]{2,0,1:T(8,128)}, f32[18,128,128]{2,0,1:T(8,128)S(1)}, u32[]{:S(2)}) copy-start(f32[18,128,128]{2,0,1:T(8,128)S(1)} %maximum_bitcast_fusion) | copy-start | bytes 3538948
  143.8 11.9 %collective-permute-start.1 = (f32[2,1,128,128]{3,1,2,0:T(1,128)S(1)}, f32[2,1,128,128]{3,1,2,0:T(1,128)S(1)}, u32[]{:S(2)}, u32[]{:S(2)}) collective-permute-start(f32[2,1,128,128]{3,1,2,0:T(1,128)S(1)} %get-tuple-element.13), channel_id=1, source_target_pairs={{32,0},{64,32},{96,64},{128,96},{160,128},{192,160},{224,192},{33,... | collective-permute-start | bytes 393224 | tf_op jit(solution)/shard_map/ppermute | solution.py:15
  149.2 10.8 %collective-permute-start = (f32[2,1,128,128]{3,1,2,0:T(1,128)S(1)}, f32[2,1,128,128]{3,1,2,0:T(1,128)S(1)}, u32[]{:S(2)}, u32[]{:S(2)}) collective-permute-start(f32[2,1,128,128]{3,1,2,0:T(1,128)S(1)} %get-tuple-element.12), channel_id=1, source_target_pairs={{0,32},{32,64},{64,96},{96,128},{128,160},{160,192},{192,224},{1,3... | collective-permute-start | bytes 393224 | tf_op jit(solution)/shard_map/ppermute | solution.py:14
  160.0 1.6 copy-start.11
  160.0 1.7 copy-start.13
  160.3 2.0 copy-start.4
  160.3 2.3 copy-start.5
  160.3 3.8 copy-start.6
  160.3 4.4 %copy-start.7 = (f32[18,128,128]{2,0,1:T(8,128)S(1)}, f32[18,128,128]{2,0,1:T(8,128)}, u32[]{:S(2)}) copy-start(f32[18,128,128]{2,0,1:T(8,128)} %get-tuple-element.39) | copy-start | bytes 3538948
  160.3 4.8 %copy-start.8 = (f32[18,128,128]{2,0,1:T(8,128)S(1)}, f32[18,128,128]{2,0,1:T(8,128)}, u32[]{:S(2)}) copy-start(f32[18,128,128]{2,0,1:T(8,128)} %get-tuple-element.40) | copy-start | bytes 3538948
  160.3 5.2 %copy-start.9 = (f32[18,128,128]{2,0,1:T(8,128)S(1)}, f32[18,128,128]{2,0,1:T(8,128)}, u32[]{:S(2)}) copy-start(f32[18,128,128]{2,0,1:T(8,128)} %get-tuple-element.41) | copy-start | bytes 3538948
  160.3 5.7 %copy-start.10 = (f32[18,128,128]{2,0,1:T(8,128)S(1)}, f32[18,128,128]{2,0,1:T(8,128)}, u32[]{:S(2)}) copy-start(f32[18,128,128]{2,0,1:T(8,128)} %get-tuple-element.42) | copy-start | bytes 3538948
  161.6 8.4 %copy-start = (f32[18,128,128]{2,0,1:T(8,128)}, f32[18,128,128]{2,0,1:T(8,128)S(1)}, u32[]{:S(2)}) copy-start(f32[18,128,128]{2,0,1:T(8,128)S(1)} %get-tuple-element.36) | copy-start | bytes 3538948
  161.6 8.4 %copy-start.1 = (f32[18,128,128]{2,0,1:T(8,128)}, f32[18,128,128]{2,0,1:T(8,128)S(1)}, u32[]{:S(2)}) copy-start(f32[18,128,128]{2,0,1:T(8,128)S(1)} %get-tuple-element.37) | copy-start | bytes 3538948
  170.1 6.3 %collective-permute-start.5 = (f32[1,1,128,128]{3,1,2,0:T(1,128)S(1)}, f32[1,1,128,128]{3,1,2,0:T(1,128)S(1)}, u32[]{:S(2)}, u32[]{:S(2)}) collective-permute-start(f32[1,1,128,128]{3,1,2,0:T(1,128)S(1)} %get-tuple-element.49), channel_id=1, source_target_pairs={{32,0},{64,32},{96,64},{128,96},{160,128},{192,160},{224,192},{33,... | collective-permute-start | bytes 196616 | tf_op jit(solution)/shard_map/ppermute | solution.py:15
  173.3 9.8 %collective-permute-start.4 = (f32[1,1,128,128]{3,1,2,0:T(1,128)S(1)}, f32[1,1,128,128]{3,1,2,0:T(1,128)S(1)}, u32[]{:S(2)}, u32[]{:S(2)}) collective-permute-start(f32[1,1,128,128]{3,1,2,0:T(1,128)S(1)} %get-tuple-element.48), channel_id=1, source_target_pairs={{0,32},{32,64},{64,96},{96,128},{128,160},{160,192},{192,224},{1,3... | collective-permute-start | bytes 196616 | tf_op jit(solution)/shard_map/ppermute | solution.py:14
  201.0 11.8 %copy-start.2 = (f32[16,128,128]{2,0,1:T(8,128)}, f32[16,128,128]{2,0,1:T(8,128)S(1)}, u32[]{:S(2)}) copy-start(f32[16,128,128]{2,0,1:T(8,128)S(1)} %fusion.49) | copy-start | bytes 3145732
  201.1 6.5 %collective-permute-start.7 = (f32[1,1,128,128]{3,1,2,0:T(1,128)S(1)}, f32[1,1,128,128]{3,1,2,0:T(1,128)S(1)}, u32[]{:S(2)}, u32[]{:S(2)}) collective-permute-start(f32[1,1,128,128]{3,1,2,0:T(1,128)S(1)} %get-tuple-element.47), channel_id=1, source_target_pairs={{32,0},{64,32},{96,64},{128,96},{160,128},{192,160},{224,192},{33,... | collective-permute-start | bytes 196616 | tf_op jit(solution)/shard_map/ppermute | solution.py:15
  203.1 9.8 %collective-permute-start.6 = (f32[1,1,128,128]{3,1,2,0:T(1,128)S(1)}, f32[1,1,128,128]{3,1,2,0:T(1,128)S(1)}, u32[]{:S(2)}, u32[]{:S(2)}) collective-permute-start(f32[1,1,128,128]{3,1,2,0:T(1,128)S(1)} %get-tuple-element.46), channel_id=1, source_target_pairs={{0,32},{32,64},{64,96},{96,128},{128,160},{160,192},{192,224},{1,3... | collective-permute-start | bytes 196616 | tf_op jit(solution)/shard_map/ppermute | solution.py:14
  230.9 6.9 %collective-permute-start.9 = (f32[1,1,128,128]{3,1,2,0:T(1,128)S(1)}, f32[1,1,128,128]{3,1,2,0:T(1,128)S(1)}, u32[]{:S(2)}, u32[]{:S(2)}) collective-permute-start(f32[1,1,128,128]{3,1,2,0:T(1,128)S(1)} %get-tuple-element.45), channel_id=1, source_target_pairs={{32,0},{64,32},{96,64},{128,96},{160,128},{192,160},{224,192},{33,... | collective-permute-start | bytes 196616 | tf_op jit(solution)/shard_map/ppermute | solution.py:15
  232.8 9.8 %collective-permute-start.8 = (f32[1,1,128,128]{3,1,2,0:T(1,128)S(1)}, f32[1,1,128,128]{3,1,2,0:T(1,128)S(1)}, u32[]{:S(2)}, u32[]{:S(2)}) collective-permute-start(f32[1,1,128,128]{3,1,2,0:T(1,128)S(1)} %get-tuple-element.44), channel_id=1, source_target_pairs={{0,32},{32,64},{64,96},{96,128},{128,160},{160,192},{192,224},{1,3... | collective-permute-start | bytes 196616 | tf_op jit(solution)/shard_map/ppermute | solution.py:14
  262.9 1.3 copy-start.12
  264.3 111.1 %copy-start.14 = (f32[16,4,128]{2,1,0:T(4,128)S(1)}, f32[16,4,128]{2,1,0:T(4,128)}, u32[]{:S(2)}) copy-start(f32[16,4,128]{2,1,0:T(4,128)} %param.12) | copy-start | bytes 98308
  264.3 111.1 %copy-start.15 = (f32[16,4,128]{2,1,0:T(4,128)S(1)}, f32[16,4,128]{2,1,0:T(4,128)}, u32[]{:S(2)}) copy-start(f32[16,4,128]{2,1,0:T(4,128)} %param.13) | copy-start | bytes 98308
Sparse Core Ops, SparseCore 0:
  10.4 65.6 all-gather.4
  78.5 63.2 all-gather.2
  263.1 112.2 reduce-scatter.1
where the time goes:
time: 388 us; the launch traced here: 383 us
  waiting for transfers between devices  249 us (64%)
  other arithmetic  69.2 us (18%)
  starting transfers between devices  32.4 us (8%)
  local copies, waits for them, and re-layouts  16.3 us (4%)
  between operations  14.8 us (4%)
    reduce_scatter x1, waiting for transfers between devices, body(): lax.psum_scatter(weighted, 'shots', scatter_dimension=1, tiled=True)  110 us
    all_gather x1, waiting for transfers between devices, body(): lax.all_gather(density, 'shots', axis=1, tiled=True)  65.7 us
    all_gather x1, waiting for transfers between devices, body(): lax.all_gather(velocity, 'shots', axis=1, tiled=True)  49.7 us
    sub x4, other arithmetic, operate(): total = total + 0.5 * (bc + ba) * (pa - pc) - 0.5 * (bb + bc) * (pc - pb)  34.5 us
    ppermute x5, waiting for transfers between devices, with_halo(): before = lax.ppermute(last, axis, up)  23.7 us
    ppermute x5, starting transfers between devices, with_halo(): after = lax.ppermute(first, axis, down)  17.7 us
    add x3, other arithmetic, body(): 2.0 * current - older + 0.08 * kappa_ext * spread  17.1 us
    ppermute x5, starting transfers between devices, with_halo(): before = lax.ppermute(last, axis, up)  14.6 us
  transfers between devices with their start and end apart: 13, of which 8 were waited for; matrix products, arithmetic and copies ran while one was open for 4% of the time, Pallas kernels for 0%

commit v1 on v0

--- a/solution.py
+++ b/solution.py
@@ -15,6 +15,47 @@
         after = lax.ppermute(first, axis, down)
         shard = jnp.concatenate([before, shard, after], axis=dim)
     return shard
+
+
+def bit_order(peers):
+    return list(range(peers.bit_length() - 1))
+
+
+def gather_rows(shard, axis, dim):
+    peers = lax.axis_size(axis)
+    me = lax.axis_index(axis)
+    pieces = jnp.expand_dims(shard, dim)
+    for b in reversed(bit_order(peers)):
+        pairs = [(i, i ^ (1 << b)) for i in range(peers)]
+        got = lax.ppermute(pieces, axis, pairs)
+        mine = (me >> b) & 1
+        lo = jnp.where(mine == 0, pieces, got)
+        hi = jnp.where(mine == 0, got, pieces)
+        both = jnp.stack([lo, hi], axis=dim + 1)
+        shape = list(pieces.shape)
+        shape[dim] = shape[dim] * 2
+        pieces = both.reshape(shape)
+    shape = list(shard.shape)
+    shape[dim] = shape[dim] * peers
+    return pieces.reshape(shape)
+
+
+def scatter_rows(full, axis, dim):
+    peers = lax.axis_size(axis)
+    me = lax.axis_index(axis)
+    nbits = peers.bit_length() - 1
+    rows = full.shape[dim] // peers
+    shape = list(full.shape)
+    blocks = full.reshape(shape[:dim] + [2] * nbits + [rows] + shape[dim + 1:])
+    for b in bit_order(peers):
+        where = dim + (nbits - 1 - b)
+        mine = (me >> b) & 1
+        keep = lax.dynamic_index_in_dim(blocks, mine, axis=where, keepdims=False)
+        send = lax.dynamic_index_in_dim(blocks, 1 - mine, axis=where, keepdims=False)
+        pairs = [(i, i ^ (1 << b)) for i in range(peers)]
+        got = lax.ppermute(send, axis, pairs)
+        blocks = keep + got
+    return blocks
 
 
 def operate(field, buoy):
@@ -50,11 +91,8 @@
     steps = fwd_snap.shape[1]
     groups = lax.axis_size("shots")
     width = 1
-    vel_all, rho_all = (
-        lax.all_gather(velocity, "shots", axis=1, tiled=True),
-        lax.all_gather(density, "shots", axis=1, tiled=True),
-    )
-    packed = jnp.stack([rho_all * vel_all * vel_all, 1.0 / rho_all])
+    local = jnp.stack([density * velocity * velocity, 1.0 / density])
+    packed = gather_rows(local, "shots", 2)
     extended = with_halo(packed, (("depth", 1),), width)
     buoy_ext = extended[1]
     first = lax.axis_index("depth") * depth_planes
@@ -79,7 +117,7 @@
         older = current
         current = newer
     weighted = shot_count[0].astype(jnp.float32) * image
-    summed = lax.psum_scatter(weighted, "shots", scatter_dimension=1, tiled=True)
+    summed = scatter_rows(weighted, "shots", 1)
     grad_vel = 2.0 * density * velocity * summed / (4.0 * groups)
     return (current[None], older[None], grad_vel)
 

time: 388 us -> 200 us (0.52); the launches traced: 383 us -> 200 us
  waiting for transfers between devices: 249 us -> 64.7 us
  starting transfers between devices: 32.4 us -> 48.3 us
  between operations: 14.8 us -> 2.06 us
    all_gather x2 -> x0, waiting for transfers between devices: 115 us -> none  [the longest x1 65.7 us: body(): lax.all_gather(density, 'shots', axis=1, tiled=True)]
    reduce_scatter x1 -> x0, waiting for transfers between devices: 110 us -> none  [body(): lax.psum_scatter(weighted, 'shots', scatter_dimension=1, tiled=True)]
    ppermute x0 -> x10, waiting for transfers between devices: none -> 40.9 us  [the longest x5 22.2 us: scatter_rows(): got = lax.ppermute(send, axis, pairs)]
    ppermute x0 -> x10, starting transfers between devices: none -> 16.4 us  [the longest x5 11.3 us: gather_rows(): got = lax.ppermute(pieces, axis, pairs)]
    unnamed x44 -> x62, local copies, waits for them, and re-layouts: 12.2 us -> 12.4 us
  transfers between devices with their start and end apart: 13 -> 20, of which waited for: 8 -> 14; matrix products, arithmetic and copies ran while one was open for 4% -> 6% of each run, Pallas kernels for 0% -> 0%
where the time goes in v1:
time: 200 us
  other arithmetic  68 us (34%)
  waiting for transfers between devices  64.7 us (32%)
  starting transfers between devices  48.3 us (24%)
  local copies, waits for them, and re-layouts  14.9 us (7%)
  between operations  2.06 us (1%)
    sub x4, other arithmetic, operate(): total = total + 0.5 * (bc + ba) * (pa - pc) - 0.5 * (bb + bc) * (pc - pb)  33.5 us
    ppermute x5, waiting for transfers between devices, with_halo(): before = lax.ppermute(last, axis, up)  23.4 us
    ppermute x5, waiting for transfers between devices, scatter_rows(): got = lax.ppermute(send, axis, pairs)  22.2 us
    ppermute x5, waiting for transfers between devices, gather_rows(): got = lax.ppermute(pieces, axis, pairs)  18.7 us
    add x3, other arithmetic, body(): 2.0 * current - older + 0.08 * kappa_ext * spread  17.1 us
    ppermute x5, starting transfers between devices, with_halo(): after = lax.ppermute(first, axis, down)  16.1 us
    ppermute x5, starting transfers between devices, with_halo(): before = lax.ppermute(last, axis, up)  15.8 us
    unnamed x62, local copies, waits for them, and re-layouts  12.4 us
  transfers between devices with their start and end apart: 20, of which 14 were waited for; matrix products, arithmetic and copies ran while one was open for 6% of the time, Pallas kernels for 0%

profile of v1, /device:TPU:24, one launch (start us, length us, event | category | flops | bytes accessed | tf_op | source)
XLA Modules:
  0.0 199.6 jit_solution(16769841357678050399)
XLA Ops:
  0.6 0.8 fusion.99
  1.4 7.3 %collective-permute-start = (f32[2,16,1,4,128]{4,1,3,0,2:T(8,128)S(1)}, f32[2,16,1,4,128]{4,1,3,0,2:T(8,128)S(1)}, u32[]{:S(2)}, u32[]{:S(2)}) collective-permute-start(f32[2,16,1,4,128]{4,1,3,0,2:T(8,128)S(1)} %maximum_bitcast_fusion.5), channel_id=1, source_target_pairs={{0,16},{1,17},{2,18},{3,19},{4,20},{5,21},{6,22},{7,23},{8,24},{9,... | collective-permute-start | bytes 196616 | tf_op jit(solution)/shard_map/ppermute | solution.py:30
  8.7 2.4 %collective-permute-done = f32[2,16,1,4,128]{4,1,3,0,2:T(8,128)S(1)} collective-permute-done((f32[2,16,1,4,128]{4,1,3,0,2:T(8,128)S(1)}, f32[2,16,1,4,128]{4,1,3,0,2:T(8,128)S(1)}, u32[]{:S(2)}, u32[]{:S(2)}) %collective-permute-start) | collective-permute-done | bytes 65568 | tf_op jit(solution)/shard_map/ppermute | solution.py:30
  11.2 3.0 %collective-permute-start.1 = (f32[2,16,2,4,128]{4,1,3,2,0:T(8,128)S(1)}, f32[2,16,2,4,128]{4,1,3,2,0:T(8,128)S(1)}, u32[]{:S(2)}, u32[]{:S(2)}) collective-permute-start(f32[2,16,2,4,128]{4,1,3,2,0:T(8,128)S(1)} %maximum_bitcast_fusion.4), channel_id=1, source_target_pairs={{0,8},{1,9},{2,10},{3,11},{4,12},{5,13},{6,14},{7,15},{8,0},{9,1},... | collective-permute-start | bytes 393224 | tf_op jit(solution)/shard_map/ppermute | solution.py:30
  14.2 5.1 %collective-permute-done.1 = f32[2,16,2,4,128]{4,1,3,2,0:T(8,128)S(1)} collective-permute-done((f32[2,16,2,4,128]{4,1,3,2,0:T(8,128)S(1)}, f32[2,16,2,4,128]{4,1,3,2,0:T(8,128)S(1)}, u32[]{:S(2)}, u32[]{:S(2)}) %collective-permute-start.1) | collective-permute-done | bytes 131104 | tf_op jit(solution)/shard_map/ppermute | solution.py:30
  19.4 7.6 %collective-permute-done.2 = f32[2,16,4,4,128]{4,1,3,2,0:T(8,128)S(1)} collective-permute-done((f32[2,16,4,4,128]{4,1,3,2,0:T(8,128)S(1)}, f32[2,16,4,4,128]{4,1,3,2,0:T(8,128)S(1)}, u32[]{:S(2)}, u32[]{:S(2)}) %collective-permute-start.2) | collective-permute-done | bytes 262176 | tf_op jit(solution)/shard_map/ppermute | solution.py:30
  27.2 0.8 collective-permute-start.3
  28.0 5.0 %collective-permute-start.8 = (f32[1,1,128,128]{3,1,2,0:T(1,128)S(1)}, f32[1,1,128,128]{3,1,2,0:T(1,128)S(1)}, u32[]{:S(2)}, u32[]{:S(2)}) collective-permute-start(f32[1,1,128,128]{3,1,2,0:T(1,128)S(1)} %bitcast.148), channel_id=1, source_target_pairs={{32,0},{64,32},{96,64},{128,96},{160,128},{192,160},{224,192},{33,... | collective-permute-start | bytes 196616 | tf_op jit(solution)/shard_map/ppermute | solution.py:15
  33.1 1.9 collective-permute-start.7
  35.0 0.6 copy.48
  35.7 0.4 fusion.81
  36.1 3.6 %collective-permute-done.3 = f32[2,16,8,4,128]{4,1,3,2,0:T(8,128)S(1)} collective-permute-done((f32[2,16,8,4,128]{4,1,3,2,0:T(8,128)S(1)}, f32[2,16,8,4,128]{4,1,3,2,0:T(8,128)S(1)}, u32[]{:S(2)}, u32[]{:S(2)}) %collective-permute-start.3) | collective-permute-done | bytes 524320 | tf_op jit(solution)/shard_map/ppermute | solution.py:30
  40.1 1.4 copy-done.22
  41.5 1.4 fusion.107
  42.9 0.2 maximum_bitcast_fusion
  43.2 4.6 %fusion.12 = (f32[18,128,128]{2,0,1:T(8,128)}, f32[18,128,128]{2,0,1:T(8,128)}, f32[18,128,128]{2,0,1:T(8,128)}, f32[18,128,128]{2,0,1:T(8,128)}, f32[18,128,128]{2,0,1:T(8,128)}, /*index=5*/f32[18,128,128]{2,0,1:T(8,128)}) fusion(f32[18,128,128]{2,0,1:T(8,128)S(1)} %maximum_bitcast_fusion), kind=kLoop, calls=%fused_computation.45 | loop fusion | flops 589824 | bytes 8257536 | tf_op jit(solution)/shard_map/sub | solution.py:73
  47.9 0.2 pad_maximum_fusion
  48.2 0.2 copy.59
  48.6 5.3 %collective-permute-start.6 = (f32[2,1,128,128]{3,1,2,0:T(1,128)S(1)}, f32[2,1,128,128]{3,1,2,0:T(1,128)S(1)}, u32[]{:S(2)}, u32[]{:S(2)}) collective-permute-start(f32[2,1,128,128]{3,1,2,0:T(1,128)S(1)} %get-tuple-element.16), channel_id=1, source_target_pairs={{32,0},{64,32},{96,64},{128,96},{160,128},{192,160},{224,192},{33,... | collective-permute-start | bytes 393224 | tf_op jit(solution)/shard_map/ppermute | solution.py:15
  53.9 1.9 collective-permute-start.5
  56.1 0.4 collective-permute-done.6
  56.4 8.0 %collective-permute-done.5 = f32[2,1,128,128]{3,1,2,0:T(1,128)S(1)} collective-permute-done((f32[2,1,128,128]{3,1,2,0:T(1,128)S(1)}, f32[2,1,128,128]{3,1,2,0:T(1,128)S(1)}, u32[]{:S(2)}, u32[]{:S(2)}) %collective-permute-start.5) | collective-permute-done | bytes 131104 | tf_op jit(solution)/shard_map/ppermute | solution.py:14
  64.7 1.3 fusion.1
  66.2 0.5 copy-done.14
  66.7 0.8 copy-done.15
  67.4 1.6 copy-done.16
  69.0 1.5 copy-done.17
  70.5 1.3 copy-done.18
  71.8 0.4 copy-done.19
  72.2 4.0 %fusion.63 = f32[16,128,128]{2,0,1:T(8,128)S(1)} fusion(f32[18,128,128]{2,0,1:T(8,128)S(1)} %copy-done.17, f32[18,128,128]{2,0,1:T(8,128)S(1)} %copy-done.16, f32[18,128,128]{2,0,1:T(8,128)S(1)} %copy-done.15, f32[18,128,128]{2,0,1:T(8,128)S(1)} %copy-done.19, f32[18,128,128]{2,0,1:T(8,128)S(1)} %copy-done.12, f32[18,128,128]{2,0,1:T(8,128)S(1)} %copy-done.18, ...), kind=kLoop, calls=%fused_computation.121 | loop fusion | flops 5505024 | bytes 17891392 | tf_op jit(solution)/shard_map/add | solution.py:114
  76.4 1.9 collective-permute-start.10
  78.3 4.1 %collective-permute-start.9 = (f32[1,1,128,128]{3,1,2,0:T(1,128)S(1)}, f32[1,1,128,128]{3,1,2,0:T(1,128)S(1)}, u32[]{:S(2)}, u32[]{:S(2)}) collective-permute-start(f32[1,1,128,128]{3,1,2,0:T(1,128)S(1)} %get-tuple-element.53), channel_id=1, source_target_pairs={{0,32},{32,64},{64,96},{96,128},{128,160},{160,192},{192,224},{1,3... | collective-permute-start | bytes 196616 | tf_op jit(solution)/shard_map/ppermute | solution.py:14
  82.4 0.4 fusion.79
  82.9 5.2 %collective-permute-done.9 = f32[1,1,128,128]{3,1,2,0:T(1,128)S(1)} collective-permute-done((f32[1,1,128,128]{3,1,2,0:T(1,128)S(1)}, f32[1,1,128,128]{3,1,2,0:T(1,128)S(1)}, u32[]{:S(2)}, u32[]{:S(2)}) %collective-permute-start.9) | collective-permute-done | bytes 65568 | tf_op jit(solution)/shard_map/ppermute | solution.py:14
  88.1 1.4 maximum_bitcast_fusion.1
  89.5 9.6 %fusion.14 = (f32[18,128,128]{2,0,1:T(8,128)}, f32[18,128,128]{2,0,1:T(8,128)}, f32[18,128,128]{2,0,1:T(8,128)}, f32[18,128,128]{2,0,1:T(8,128)}, f32[18,128,128]{2,0,1:T(8,128)}, /*index=5*/f32[18,128,128]{2,0,1:T(8,128)}) fusion(f32[18,128,128]{2,0,1:T(8,128)} %maximum_bitcast_fusion.1), kind=kLoop, calls=%fused_computation.47 | loop fusion | flops 589824 | bytes 8257536 | tf_op jit(solution)/shard_map/sub | solution.py:73
  99.1 6.6 %fusion.51 = f32[16,128,128]{2,0,1:T(8,128)S(1)} fusion(f32[18,128,128]{2,0,1:T(8,128)} %get-tuple-element.34, f32[18,128,128]{2,0,1:T(8,128)} %get-tuple-element.33, f32[18,128,128]{2,0,1:T(8,128)} %get-tuple-element.32, f32[18,128,128]{2,0,1:T(8,128)} %get-tuple-element.36, f32[18,128,128]{2,0,1:T(8,128)} %maximum_bitcast_fusion.1, ...), kind=kLoop, calls=%fused_computation.103 | loop fusion | flops 5505024 | bytes 17891392 | tf_op jit(solution)/shard_map/add | solution.py:114
  105.9 1.9 collective-permute-start.12
  107.8 3.9 %collective-permute-start.11 = (f32[1,1,128,128]{3,1,2,0:T(1,128)S(1)}, f32[1,1,128,128]{3,1,2,0:T(1,128)S(1)}, u32[]{:S(2)}, u32[]{:S(2)}) collective-permute-start(f32[1,1,128,128]{3,1,2,0:T(1,128)S(1)} %get-tuple-element.51), channel_id=1, source_target_pairs={{0,32},{32,64},{64,96},{96,128},{128,160},{160,192},{192,224},{1,3... | collective-permute-start | bytes 196616 | tf_op jit(solution)/shard_map/ppermute | solution.py:14
  111.7 0.4 fusion.77
  112.2 5.4 %collective-permute-done.11 = f32[1,1,128,128]{3,1,2,0:T(1,128)S(1)} collective-permute-done((f32[1,1,128,128]{3,1,2,0:T(1,128)S(1)}, f32[1,1,128,128]{3,1,2,0:T(1,128)S(1)}, u32[]{:S(2)}, u32[]{:S(2)}) %collective-permute-start.11) | collective-permute-done | bytes 65568 | tf_op jit(solution)/shard_map/ppermute | solution.py:14
  117.6 1.4 maximum_bitcast_fusion.2
  119.0 9.6 %fusion.16 = (f32[18,128,128]{2,0,1:T(8,128)}, f32[18,128,128]{2,0,1:T(8,128)}, f32[18,128,128]{2,0,1:T(8,128)}, f32[18,128,128]{2,0,1:T(8,128)}, f32[18,128,128]{2,0,1:T(8,128)}, /*index=5*/f32[18,128,128]{2,0,1:T(8,128)}) fusion(f32[18,128,128]{2,0,1:T(8,128)} %maximum_bitcast_fusion.2), kind=kLoop, calls=%fused_computation.49 | loop fusion | flops 589824 | bytes 8257536 | tf_op jit(solution)/shard_map/sub | solution.py:73
  128.7 6.4 %fusion.39 = f32[16,128,128]{2,0,1:T(8,128)S(1)} fusion(f32[18,128,128]{2,0,1:T(8,128)} %get-tuple-element.28, f32[18,128,128]{2,0,1:T(8,128)} %get-tuple-element.27, f32[18,128,128]{2,0,1:T(8,128)} %get-tuple-element.26, f32[18,128,128]{2,0,1:T(8,128)} %get-tuple-element.30, f32[18,128,128]{2,0,1:T(8,128)} %maximum_bitcast_fusion.2, ...), kind=kLoop, calls=%fused_computation.85 | loop fusion | flops 5505024 | bytes 17891392 | tf_op jit(solution)/shard_map/add | solution.py:114
  135.2 1.9 collective-permute-start.14
  137.1 3.9 %collective-permute-start.13 = (f32[1,1,128,128]{3,1,2,0:T(1,128)S(1)}, f32[1,1,128,128]{3,1,2,0:T(1,128)S(1)}, u32[]{:S(2)}, u32[]{:S(2)}) collective-permute-start(f32[1,1,128,128]{3,1,2,0:T(1,128)S(1)} %get-tuple-element.49), channel_id=1, source_target_pairs={{0,32},{32,64},{64,96},{96,128},{128,160},{160,192},{192,224},{1,3... | collective-permute-start | bytes 196616 | tf_op jit(solution)/shard_map/ppermute | solution.py:14
  141.1 0.4 fusion.75
  142.1 4.8 %collective-permute-done.13 = f32[1,1,128,128]{3,1,2,0:T(1,128)S(1)} collective-permute-done((f32[1,1,128,128]{3,1,2,0:T(1,128)S(1)}, f32[1,1,128,128]{3,1,2,0:T(1,128)S(1)}, u32[]{:S(2)}, u32[]{:S(2)}) %collective-permute-start.13) | collective-permute-done | bytes 65568 | tf_op jit(solution)/shard_map/ppermute | solution.py:14
  146.9 1.4 maximum_bitcast_fusion.3
  148.3 9.7 %fusion.18 = (f32[18,128,128]{2,0,1:T(8,128)}, f32[18,128,128]{2,0,1:T(8,128)}, f32[18,128,128]{2,0,1:T(8,128)}, f32[18,128,128]{2,0,1:T(8,128)}, f32[18,128,128]{2,0,1:T(8,128)}, /*index=5*/f32[18,128,128]{2,0,1:T(8,128)}) fusion(f32[18,128,128]{2,0,1:T(8,128)} %maximum_bitcast_fusion.3), kind=kLoop, calls=%fused_computation.51 | loop fusion | flops 589824 | bytes 8257536 | tf_op jit(solution)/shard_map/sub | solution.py:73
  158.0 8.7 %fusion.72 = (f32[16,128,128]{2,0,1:T(8,128)S(1)}, f32[16,128,128]{2,0,1:T(8,128)}) fusion(f32[16,128,128]{2,0,1:T(8,128)S(1)} %fusion.39, f32[16,128,128]{2,0,1:T(8,128)} %copy-done.10, f32[16,128,128]{2,0,1:T(8,128)S(1)} %fusion.63, bf16[1,1,16,128,128]{4,3,2,1,0:T(8,128)(2,1)} %get-tuple-element.14, bf16[1,1,16,128,128]{4,3,2,1,0:T(8,128)(2,1)} %get-tuple-element.12, ...), kind=kLoop, calls=%fused_computation.137 | loop fusion | flops 8650752 | bytes 22085700 | tf_op jit(solution)/shard_map/mul | solution.py:119
  166.7 1.0 copy-done.21
  167.8 1.9 collective-permute-done.15
  169.7 1.1 bitcast_add_fusion
  170.9 0.3 collective-permute-start.16
  171.2 8.3 %collective-permute-done.16 = f32[16,2,2,2,4,128]{5,0,4,3,2,1:T(8,128)S(1)} collective-permute-done((f32[16,2,2,2,4,128]{5,0,4,3,2,1:T(8,128)S(1)}, f32[16,2,2,2,4,128]{5,0,4,3,2,1:T(8,128)S(1)}, u32[]{:S(2)}, u32[]{:S(2)}) %collective-permute-start.16) | collective-permute-done | bytes 262176 | tf_op jit(solution)/shard_map/ppermute | solution.py:56
  179.6 0.7 collective-permute-start.17
  180.3 4.4 %collective-permute-done.17 = f32[16,2,2,4,128]{4,0,3,2,1:T(8,128)S(1)} collective-permute-done((f32[16,2,2,4,128]{4,0,3,2,1:T(8,128)S(1)}, f32[16,2,2,4,128]{4,0,3,2,1:T(8,128)S(1)}, u32[]{:S(2)}, u32[]{:S(2)}) %collective-permute-start.17) | collective-permute-done | bytes 131104 | tf_op jit(solution)/shard_map/ppermute | solution.py:56
  184.8 5.9 %collective-permute-done.18 = f32[16,2,4,128]{3,0,2,1:T(8,128)S(1)} collective-permute-done((f32[16,2,4,128]{3,0,2,1:T(8,128)S(1)}, f32[16,2,4,128]{3,0,2,1:T(8,128)S(1)}, u32[]{:S(2)}, u32[]{:S(2)}) %collective-permute-start.18) | collective-permute-done | bytes 65568 | tf_op jit(solution)/shard_map/ppermute | solution.py:56
  190.7 3.9 %collective-permute-start.19 = (f32[16,4,128]{2,0,1:T(8,128)S(1)}, f32[16,4,128]{2,0,1:T(8,128)S(1)}, u32[]{:S(2)}, u32[]{:S(2)}) collective-permute-start(f32[16,4,128]{2,0,1:T(8,128)S(1)} %dynamic-slice_bitcast_fusion.4), channel_id=1, source_target_pairs={{0,16},{1,17},{2,18},{3,19},{4,20},{5,21},{6,22},{7,23},{8,24},{9,... | collective-permute-start | bytes 98312 | tf_op jit(solution)/shard_map/ppermute | solution.py:56
  194.6 1.3 copy.70
  195.9 1.3 copy.69
  197.2 1.7 collective-permute-done.19
  198.9 0.6 copy.71
  (91 shorter events, 2.3 us)
Async XLA Ops:
  1.4 9.7 %collective-permute-start = (f32[2,16,1,4,128]{4,1,3,0,2:T(8,128)S(1)}, f32[2,16,1,4,128]{4,1,3,0,2:T(8,128)S(1)}, u32[]{:S(2)}, u32[]{:S(2)}) collective-permute-start(f32[2,16,1,4,128]{4,1,3,0,2:T(8,128)S(1)} %maximum_bitcast_fusion.5), channel_id=1, source_target_pairs={{0,16},{1,17},{2,18},{3,19},{4,20},{5,21},{6,22},{7,23},{8,24},{9,... | collective-permute-start | bytes 196616 | tf_op jit(solution)/shard_map/ppermute | solution.py:30
  11.2 8.1 %collective-permute-start.1 = (f32[2,16,2,4,128]{4,1,3,2,0:T(8,128)S(1)}, f32[2,16,2,4,128]{4,1,3,2,0:T(8,128)S(1)}, u32[]{:S(2)}, u32[]{:S(2)}) collective-permute-start(f32[2,16,2,4,128]{4,1,3,2,0:T(8,128)S(1)} %maximum_bitcast_fusion.4), channel_id=1, source_target_pairs={{0,8},{1,9},{2,10},{3,11},{4,12},{5,13},{6,14},{7,15},{8,0},{9,1},... | collective-permute-start | bytes 393224 | tf_op jit(solution)/shard_map/ppermute | solution.py:30
  19.3 7.7 %collective-permute-start.2 = (f32[2,16,4,4,128]{4,1,3,2,0:T(8,128)S(1)}, f32[2,16,4,4,128]{4,1,3,2,0:T(8,128)S(1)}, u32[]{:S(2)}, u32[]{:S(2)}) collective-permute-start(f32[2,16,4,4,128]{4,1,3,2,0:T(8,128)S(1)} %bitcast.145), channel_id=1, source_target_pairs={{0,4},{1,5},{2,6},{3,7},{4,0},{5,1},{6,2},{7,3},{8,12},{9,13},{10,... | collective-permute-start | bytes 786440 | tf_op jit(solution)/shard_map/ppermute | solution.py:30
  19.4 8.6 %copy-start.13 = (f32[1,16,128,128]{3,2,1,0:T(8,128)S(1)}, f32[1,16,128,128]{3,2,1,0:T(8,128)}, u32[]{:S(2)}) copy-start(f32[1,16,128,128]{3,2,1,0:T(8,128)} %param.9) | copy-start | bytes 3145732
  27.1 8.5 %copy-start.26 = (f32[1,4,256]{2,1,0:T(4,128)S(1)}, f32[1,4,256]{2,1,0:T(4,128)}, u32[]{:S(2)}) copy-start(f32[1,4,256]{2,1,0:T(4,128)} %param.17) | copy-start | bytes 12292
  27.1 8.6 %copy-start.27 = (s32[1,256]{1,0:T(1,128)S(1)}, s32[1,256]{1,0:T(1,128)}, u32[]{:S(2)}) copy-start(s32[1,256]{1,0:T(1,128)} %param.16) | copy-start | bytes 3076
  27.1 8.6 %copy-start.28 = (s32[1,256]{1,0:T(1,128)S(1)}, s32[1,256]{1,0:T(1,128)}, u32[]{:S(2)}) copy-start(s32[1,256]{1,0:T(1,128)} %param.15) | copy-start | bytes 3076
  27.2 12.5 %collective-permute-start.3 = (f32[2,16,8,4,128]{4,1,3,2,0:T(8,128)S(1)}, f32[2,16,8,4,128]{4,1,3,2,0:T(8,128)S(1)}, u32[]{:S(2)}, u32[]{:S(2)}) collective-permute-start(f32[2,16,8,4,128]{4,1,3,2,0:T(8,128)S(1)} %bitcast.143), channel_id=1, source_target_pairs={{0,2},{1,3},{2,0},{3,1},{4,6},{5,7},{6,4},{7,5},{8,10},{9,11},{10,... | collective-permute-start | bytes 1572872 | tf_op jit(solution)/shard_map/ppermute | solution.py:30
  28.0 14.8 %collective-permute-start.8 = (f32[1,1,128,128]{3,1,2,0:T(1,128)S(1)}, f32[1,1,128,128]{3,1,2,0:T(1,128)S(1)}, u32[]{:S(2)}, u32[]{:S(2)}) collective-permute-start(f32[1,1,128,128]{3,1,2,0:T(1,128)S(1)} %bitcast.148), channel_id=1, source_target_pairs={{32,0},{64,32},{96,64},{128,96},{160,128},{192,160},{224,192},{33,... | collective-permute-start | bytes 196616 | tf_op jit(solution)/shard_map/ppermute | solution.py:15
  33.1 9.8 %collective-permute-start.7 = (f32[1,1,128,128]{3,1,2,0:T(1,128)S(1)}, f32[1,1,128,128]{3,1,2,0:T(1,128)S(1)}, u32[]{:S(2)}, u32[]{:S(2)}) collective-permute-start(f32[1,1,128,128]{3,1,2,0:T(1,128)S(1)} %bitcast.147), channel_id=1, source_target_pairs={{0,32},{32,64},{64,96},{96,128},{128,160},{160,192},{192,224},{1,3... | collective-permute-start | bytes 196616 | tf_op jit(solution)/shard_map/ppermute | solution.py:14
  39.9 1.6 copy-start.22
  40.0 7.7 %collective-permute-start.4 = (f32[2,16,16,4,128]{4,1,3,2,0:T(8,128)S(1)}, f32[2,16,16,4,128]{4,1,3,2,0:T(8,128)S(1)}, u32[]{:S(2)}, u32[]{:S(2)}) collective-permute-start(f32[2,16,16,4,128]{4,1,3,2,0:T(8,128)S(1)} %bitcast.141), channel_id=1, source_target_pairs={{0,1},{1,0},{2,3},{3,2},{4,5},{5,4},{6,7},{7,6},{8,9},{9,8},{10,11... | collective-permute-start | bytes 3145736 | tf_op jit(solution)/shard_map/ppermute | solution.py:30
  43.2 4.6 %copy-start.11 = (f32[18,128,128]{2,0,1:T(8,128)}, f32[18,128,128]{2,0,1:T(8,128)S(1)}, u32[]{:S(2)}) copy-start(f32[18,128,128]{2,0,1:T(8,128)S(1)} %maximum_bitcast_fusion) | copy-start | bytes 3538948
  48.6 7.8 %collective-permute-start.6 = (f32[2,1,128,128]{3,1,2,0:T(1,128)S(1)}, f32[2,1,128,128]{3,1,2,0:T(1,128)S(1)}, u32[]{:S(2)}, u32[]{:S(2)}) collective-permute-start(f32[2,1,128,128]{3,1,2,0:T(1,128)S(1)} %get-tuple-element.16), channel_id=1, source_target_pairs={{32,0},{64,32},{96,64},{128,96},{160,128},{192,160},{224,192},{33,... | collective-permute-start | bytes 393224 | tf_op jit(solution)/shard_map/ppermute | solution.py:15
  53.9 10.5 %collective-permute-start.5 = (f32[2,1,128,128]{3,1,2,0:T(1,128)S(1)}, f32[2,1,128,128]{3,1,2,0:T(1,128)S(1)}, u32[]{:S(2)}, u32[]{:S(2)}) collective-permute-start(f32[2,1,128,128]{3,1,2,0:T(1,128)S(1)} %get-tuple-element.15), channel_id=1, source_target_pairs={{0,32},{32,64},{64,96},{96,128},{128,160},{160,192},{192,224},{1,3... | collective-permute-start | bytes 393224 | tf_op jit(solution)/shard_map/ppermute | solution.py:14
  64.4 1.7 copy-start.23
  64.7 1.5 copy-start.12
  64.7 2.0 %copy-start.14 = (f32[18,128,128]{2,0,1:T(8,128)S(1)}, f32[18,128,128]{2,0,1:T(8,128)}, u32[]{:S(2)}) copy-start(f32[18,128,128]{2,0,1:T(8,128)} %get-tuple-element.43) | copy-start | bytes 3538948
  64.7 2.8 %copy-start.15 = (f32[18,128,128]{2,0,1:T(8,128)S(1)}, f32[18,128,128]{2,0,1:T(8,128)}, u32[]{:S(2)}) copy-start(f32[18,128,128]{2,0,1:T(8,128)} %get-tuple-element.44) | copy-start | bytes 3538948
  64.7 4.3 %copy-start.16 = (f32[18,128,128]{2,0,1:T(8,128)S(1)}, f32[18,128,128]{2,0,1:T(8,128)}, u32[]{:S(2)}) copy-start(f32[18,128,128]{2,0,1:T(8,128)} %get-tuple-element.45) | copy-start | bytes 3538948
  64.7 5.8 %copy-start.17 = (f32[18,128,128]{2,0,1:T(8,128)S(1)}, f32[18,128,128]{2,0,1:T(8,128)}, u32[]{:S(2)}) copy-start(f32[18,128,128]{2,0,1:T(8,128)} %get-tuple-element.46) | copy-start | bytes 3538948
  64.7 7.1 %copy-start.18 = (f32[18,128,128]{2,0,1:T(8,128)S(1)}, f32[18,128,128]{2,0,1:T(8,128)}, u32[]{:S(2)}) copy-start(f32[18,128,128]{2,0,1:T(8,128)} %get-tuple-element.47) | copy-start | bytes 3538948
  64.7 7.5 %copy-start.19 = (f32[18,128,128]{2,0,1:T(8,128)S(1)}, f32[18,128,128]{2,0,1:T(8,128)}, u32[]{:S(2)}) copy-start(f32[18,128,128]{2,0,1:T(8,128)} %get-tuple-element.48) | copy-start | bytes 3538948
  66.0 10.3 %copy-start.8 = (f32[18,128,128]{2,0,1:T(8,128)}, f32[18,128,128]{2,0,1:T(8,128)S(1)}, u32[]{:S(2)}) copy-start(f32[18,128,128]{2,0,1:T(8,128)S(1)} %get-tuple-element.41) | copy-start | bytes 3538948
  66.0 10.3 %copy-start.9 = (f32[18,128,128]{2,0,1:T(8,128)}, f32[18,128,128]{2,0,1:T(8,128)S(1)}, u32[]{:S(2)}) copy-start(f32[18,128,128]{2,0,1:T(8,128)S(1)} %get-tuple-element.42) | copy-start | bytes 3538948
  66.0 62.6 %copy-start = (f32[18,128,128]{2,0,1:T(8,128)}, f32[18,128,128]{2,0,1:T(8,128)S(1)}, u32[]{:S(2)}) copy-start(f32[18,128,128]{2,0,1:T(8,128)S(1)} %get-tuple-element.37) | copy-start | bytes 3538948
  66.0 62.6 %copy-start.2 = (f32[18,128,128]{2,0,1:T(8,128)}, f32[18,128,128]{2,0,1:T(8,128)S(1)}, u32[]{:S(2)}) copy-start(f32[18,128,128]{2,0,1:T(8,128)S(1)} %get-tuple-element.38) | copy-start | bytes 3538948
  66.0 62.6 %copy-start.4 = (f32[18,128,128]{2,0,1:T(8,128)}, f32[18,128,128]{2,0,1:T(8,128)S(1)}, u32[]{:S(2)}) copy-start(f32[18,128,128]{2,0,1:T(8,128)S(1)} %get-tuple-element.39) | copy-start | bytes 3538948
  66.1 62.6 %copy-start.6 = (f32[18,128,128]{2,0,1:T(8,128)}, f32[18,128,128]{2,0,1:T(8,128)S(1)}, u32[]{:S(2)}) copy-start(f32[18,128,128]{2,0,1:T(8,128)S(1)} %get-tuple-element.40) | copy-start | bytes 3538948
  76.4 6.5 %collective-permute-start.10 = (f32[1,1,128,128]{3,1,2,0:T(1,128)S(1)}, f32[1,1,128,128]{3,1,2,0:T(1,128)S(1)}, u32[]{:S(2)}, u32[]{:S(2)}) collective-permute-start(f32[1,1,128,128]{3,1,2,0:T(1,128)S(1)} %get-tuple-element.54), channel_id=1, source_target_pairs={{32,0},{64,32},{96,64},{128,96},{160,128},{192,160},{224,192},{33,... | collective-permute-start | bytes 196616 | tf_op jit(solution)/shard_map/ppermute | solution.py:15
  78.3 9.8 %collective-permute-start.9 = (f32[1,1,128,128]{3,1,2,0:T(1,128)S(1)}, f32[1,1,128,128]{3,1,2,0:T(1,128)S(1)}, u32[]{:S(2)}, u32[]{:S(2)}) collective-permute-start(f32[1,1,128,128]{3,1,2,0:T(1,128)S(1)} %get-tuple-element.53), channel_id=1, source_target_pairs={{0,32},{32,64},{64,96},{96,128},{128,160},{160,192},{192,224},{1,3... | collective-permute-start | bytes 196616 | tf_op jit(solution)/shard_map/ppermute | solution.py:14
  105.8 22.9 %copy-start.10 = (f32[16,128,128]{2,0,1:T(8,128)}, f32[16,128,128]{2,0,1:T(8,128)S(1)}, u32[]{:S(2)}) copy-start(f32[16,128,128]{2,0,1:T(8,128)S(1)} %fusion.51) | copy-start | bytes 3145732
  105.9 6.3 %collective-permute-start.12 = (f32[1,1,128,128]{3,1,2,0:T(1,128)S(1)}, f32[1,1,128,128]{3,1,2,0:T(1,128)S(1)}, u32[]{:S(2)}, u32[]{:S(2)}) collective-permute-start(f32[1,1,128,128]{3,1,2,0:T(1,128)S(1)} %get-tuple-element.52), channel_id=1, source_target_pairs={{32,0},{64,32},{96,64},{128,96},{160,128},{192,160},{224,192},{33,... | collective-permute-start | bytes 196616 | tf_op jit(solution)/shard_map/ppermute | solution.py:15
  107.8 9.8 %collective-permute-start.11 = (f32[1,1,128,128]{3,1,2,0:T(1,128)S(1)}, f32[1,1,128,128]{3,1,2,0:T(1,128)S(1)}, u32[]{:S(2)}, u32[]{:S(2)}) collective-permute-start(f32[1,1,128,128]{3,1,2,0:T(1,128)S(1)} %get-tuple-element.51), channel_id=1, source_target_pairs={{0,32},{32,64},{64,96},{96,128},{128,160},{160,192},{192,224},{1,3... | collective-permute-start | bytes 196616 | tf_op jit(solution)/shard_map/ppermute | solution.py:14
  135.2 6.9 %collective-permute-start.14 = (f32[1,1,128,128]{3,1,2,0:T(1,128)S(1)}, f32[1,1,128,128]{3,1,2,0:T(1,128)S(1)}, u32[]{:S(2)}, u32[]{:S(2)}) collective-permute-start(f32[1,1,128,128]{3,1,2,0:T(1,128)S(1)} %get-tuple-element.50), channel_id=1, source_target_pairs={{32,0},{64,32},{96,64},{128,96},{160,128},{192,160},{224,192},{33,... | collective-permute-start | bytes 196616 | tf_op jit(solution)/shard_map/ppermute | solution.py:15
  137.1 9.8 %collective-permute-start.13 = (f32[1,1,128,128]{3,1,2,0:T(1,128)S(1)}, f32[1,1,128,128]{3,1,2,0:T(1,128)S(1)}, u32[]{:S(2)}, u32[]{:S(2)}) collective-permute-start(f32[1,1,128,128]{3,1,2,0:T(1,128)S(1)} %get-tuple-element.49), channel_id=1, source_target_pairs={{0,32},{32,64},{64,96},{96,128},{128,160},{160,192},{192,224},{1,3... | collective-permute-start | bytes 196616 | tf_op jit(solution)/shard_map/ppermute | solution.py:14
  148.3 9.7 %copy-start.1 = (f32[18,128,128]{2,0,1:T(8,128)S(1)}, f32[18,128,128]{2,0,1:T(8,128)}, u32[]{:S(2)}) copy-start(f32[18,128,128]{2,0,1:T(8,128)} %copy-done) | copy-start | bytes 3538948
  148.3 9.7 %copy-start.3 = (f32[18,128,128]{2,0,1:T(8,128)S(1)}, f32[18,128,128]{2,0,1:T(8,128)}, u32[]{:S(2)}) copy-start(f32[18,128,128]{2,0,1:T(8,128)} %copy-done.2) | copy-start | bytes 3538948
  148.3 9.7 %copy-start.5 = (f32[18,128,128]{2,0,1:T(8,128)S(1)}, f32[18,128,128]{2,0,1:T(8,128)}, u32[]{:S(2)}) copy-start(f32[18,128,128]{2,0,1:T(8,128)} %copy-done.4) | copy-start | bytes 3538948
  148.3 9.7 %copy-start.7 = (f32[18,128,128]{2,0,1:T(8,128)S(1)}, f32[18,128,128]{2,0,1:T(8,128)}, u32[]{:S(2)}) copy-start(f32[18,128,128]{2,0,1:T(8,128)} %copy-done.6) | copy-start | bytes 3538948
  166.7 1.0 copy-start.21
  167.7 2.0 %collective-permute-start.15 = (f32[16,2,2,2,2,4,128]{6,0,5,4,3,2,1:T(8,128)S(1)}, f32[16,2,2,2,2,4,128]{6,0,5,4,3,2,1:T(8,128)S(1)}, u32[]{:S(2)}, u32[]{:S(2)}) collective-permute-start(f32[16,2,2,2,2,4,128]{6,0,5,4,3,2,1:T(8,128)S(1)} %dynamic-slice_bitcast_fusion), channel_id=1, source_target_pairs={{0,1},{1,0},{2,3},{3,2},{4,5},{5,4},{6,7},{7,6},{8,9},{9,8},{10,11... | collective-permute-start | bytes 1572872 | tf_op jit(solution)/shard_map/ppermute | solution.py:56
  170.9 8.7 %collective-permute-start.16 = (f32[16,2,2,2,4,128]{5,0,4,3,2,1:T(8,128)S(1)}, f32[16,2,2,2,4,128]{5,0,4,3,2,1:T(8,128)S(1)}, u32[]{:S(2)}, u32[]{:S(2)}) collective-permute-start(f32[16,2,2,2,4,128]{5,0,4,3,2,1:T(8,128)S(1)} %dynamic-slice_bitcast_fusion.1), channel_id=1, source_target_pairs={{0,2},{1,3},{2,0},{3,1},{4,6},{5,7},{6,4},{7,5},{8,10},{9,11},{10,... | collective-permute-start | bytes 786440 | tf_op jit(solution)/shard_map/ppermute | solution.py:56
  179.6 16.4 %copy-start.20 = (f32[16,128,128]{2,0,1:T(8,128)S(1)}, f32[16,128,128]{2,0,1:T(8,128)}, u32[]{:S(2)}) copy-start(f32[16,128,128]{2,0,1:T(8,128)} %get-tuple-element.10) | copy-start | bytes 3145732
  179.6 5.1 %collective-permute-start.17 = (f32[16,2,2,4,128]{4,0,3,2,1:T(8,128)S(1)}, f32[16,2,2,4,128]{4,0,3,2,1:T(8,128)S(1)}, u32[]{:S(2)}, u32[]{:S(2)}) collective-permute-start(f32[16,2,2,4,128]{4,0,3,2,1:T(8,128)S(1)} %dynamic-slice_bitcast_fusion.2), channel_id=1, source_target_pairs={{0,4},{1,5},{2,6},{3,7},{4,0},{5,1},{6,2},{7,3},{8,12},{9,13},{10,... | collective-permute-start | bytes 393224 | tf_op jit(solution)/shard_map/ppermute | solution.py:56
  184.7 6.0 %collective-permute-start.18 = (f32[16,2,4,128]{3,0,2,1:T(8,128)S(1)}, f32[16,2,4,128]{3,0,2,1:T(8,128)S(1)}, u32[]{:S(2)}, u32[]{:S(2)}) collective-permute-start(f32[16,2,4,128]{3,0,2,1:T(8,128)S(1)} %dynamic-slice_bitcast_fusion.3), channel_id=1, source_target_pairs={{0,8},{1,9},{2,10},{3,11},{4,12},{5,13},{6,14},{7,15},{8,0},{9,1},... | collective-permute-start | bytes 196616 | tf_op jit(solution)/shard_map/ppermute | solution.py:56
  190.7 8.2 %collective-permute-start.19 = (f32[16,4,128]{2,0,1:T(8,128)S(1)}, f32[16,4,128]{2,0,1:T(8,128)S(1)}, u32[]{:S(2)}, u32[]{:S(2)}) collective-permute-start(f32[16,4,128]{2,0,1:T(8,128)S(1)} %dynamic-slice_bitcast_fusion.4), channel_id=1, source_target_pairs={{0,16},{1,17},{2,18},{3,19},{4,20},{5,21},{6,22},{7,23},{8,24},{9,... | collective-permute-start | bytes 98312 | tf_op jit(solution)/shard_map/ppermute | solution.py:56
  195.9 3.0 %copy-start.24 = (f32[16,4,128]{2,1,0:T(4,128)S(1)}, f32[16,4,128]{2,1,0:T(4,128)}, u32[]{:S(2)}) copy-start(f32[16,4,128]{2,1,0:T(4,128)} %param.12) | copy-start | bytes 98308
  195.9 3.0 %copy-start.25 = (f32[16,4,128]{2,1,0:T(4,128)S(1)}, f32[16,4,128]{2,1,0:T(4,128)}, u32[]{:S(2)}) copy-start(f32[16,4,128]{2,1,0:T(4,128)} %param.13) | copy-start | bytes 98308

commit v2 on v1

--- a/solution.py
+++ b/solution.py
@@ -2,6 +2,113 @@
 import jax.numpy as jnp
 from jax import lax
 from jax.sharding import PartitionSpec as P
+from jax.experimental import pallas as pl
+from jax.experimental.pallas import tpu as pltpu
+
+INTERPRET = False
+
+HALO = 4
+
+
+def shift_fwd(v, axis, n):
+    r = pltpu.roll(v, n - 1, axis)
+    idx = lax.broadcasted_iota(jnp.int32, v.shape, axis)
+    return jnp.where(idx == n - 1, 0.0, r)
+
+
+def shift_bwd(v, axis, n):
+    r = pltpu.roll(v, 1, axis)
+    idx = lax.broadcasted_iota(jnp.int32, v.shape, axis)
+    return jnp.where(idx == 0, 0.0, r)
+
+
+def term(bc, ba, bb, pc, pa, pb):
+    return 0.5 * (bc + ba) * (pa - pc) - 0.5 * (bb + bc) * (pc - pb)
+
+
+def stencil_kernel(count_ref, adj_ref, mat_ref, snap_ref, src_ref, now_ref, prev_ref, img_ref, pbuf, qbuf):
+    ext = adj_ref.shape[1]
+    nx, ny = adj_ref.shape[2], adj_ref.shape[3]
+    steps = snap_ref.shape[0]
+    count = count_ref[0]
+
+    def one_step(step, cur, old, dst, lo, hi):
+        moment = steps - 1 - step
+
+        def plane(e, carry):
+            pc = cur(e)
+            pa = cur(e + 1)
+            pb = cur(e - 1)
+            bc = mat_ref[1, e]
+            ba = mat_ref[1, e + 1]
+            bb = mat_ref[1, e - 1]
+            total = term(bc, ba, bb, pc, pa, pb)
+            total = total + term(bc, shift_fwd(bc, 0, nx), shift_bwd(bc, 0, nx),
+                                 pc, shift_fwd(pc, 0, nx), shift_bwd(pc, 0, nx))
+            total = total + term(bc, shift_fwd(bc, 1, ny), shift_bwd(bc, 1, ny),
+                                 pc, shift_fwd(pc, 1, ny), shift_bwd(pc, 1, ny))
+            weight = jnp.where(e == HALO + 2, 1.0, 0.0)
+            new = 2.0 * pc - old(e) + 0.08 * mat_ref[0, e] * total + 0.08 * src_ref[moment] * weight
+            dst(e, new)
+            inner = jnp.logical_and(e >= HALO, e < ext - HALO)
+
+            @pl.when(inner)
+            def _():
+                z = e - HALO
+                gained = snap_ref[moment, z].astype(jnp.float32) * new
+                if step == 0:
+                    img_ref[z] = gained
+                elif step == steps - 1:
+                    img_ref[z] = count * (img_ref[z] + gained)
+                else:
+                    img_ref[z] = img_ref[z] + gained
+            return carry
+
+        lax.fori_loop(lo, hi, plane, 0)
+
+    def rd(ref, k=None):
+        if k is None:
+            return lambda e: ref[e]
+        return lambda e: ref[k, e]
+
+    def wr(ref):
+        def f(e, v):
+            ref[e] = v
+        return f
+
+    def wr_inner(ref, out):
+        def f(e, v):
+            ref[e] = v
+            @pl.when(jnp.logical_and(e >= HALO, e < ext - HALO))
+            def _():
+                out[e - HALO] = v
+        return f
+
+    def wr_out(out):
+        def f(e, v):
+            out[e - HALO] = v
+        return f
+
+    one_step(0, rd(adj_ref, 0), rd(adj_ref, 1), wr(pbuf), 1, ext - 1)
+    one_step(1, rd(pbuf), rd(adj_ref, 0), wr(qbuf), 2, ext - 2)
+    one_step(2, rd(qbuf), rd(pbuf), wr_inner(pbuf, prev_ref), 3, ext - 3)
+    one_step(3, rd(pbuf), rd(qbuf), wr_out(now_ref), HALO, ext - HALO)
+
+
+def run_steps(count, adj_ext, mat_ext, snaps, src):
+    ext, nx, ny = adj_ext.shape[1:]
+    planes = ext - 2 * HALO
+    vmem = pltpu.VMEM
+    out_shape = [jax.ShapeDtypeStruct((planes, nx, ny), jnp.float32)] * 3
+    return pl.pallas_call(
+        stencil_kernel,
+        out_shape=out_shape,
+        in_specs=[pl.BlockSpec(memory_space=pltpu.SMEM)] + [pl.BlockSpec(memory_space=vmem)] * 4,
+        out_specs=[pl.BlockSpec(memory_space=vmem)] * 3,
+        scratch_shapes=[pltpu.VMEM((ext, nx, ny), jnp.float32)] * 2,
+        compiler_params=pltpu.CompilerParams(vmem_limit_bytes=48 * 1024 * 1024),
+        interpret=INTERPRET,
+    )(count, adj_ext, mat_ext, snaps, src)
 
 
 def with_halo(shard, sides, width):
@@ -85,38 +192,20 @@
 
 
 def body(adj_now, adj_prev, fwd_snap, velocity, density, shot_count, rec_x, rec_y, residual):
-    depth_planes = adj_now.shape[1]
     width_x = adj_now.shape[2]
     width_y = adj_now.shape[3]
     steps = fwd_snap.shape[1]
     groups = lax.axis_size("shots")
-    width = 1
     local = jnp.stack([density * velocity * velocity, 1.0 / density])
     packed = gather_rows(local, "shots", 2)
-    extended = with_halo(packed, (("depth", 1),), width)
-    buoy_ext = extended[1]
-    first = lax.axis_index("depth") * depth_planes
-    snaps = fwd_snap[0]
-    rows_x = rec_x[0]
-    rows_y = rec_y[0]
-    image = jnp.zeros((depth_planes, width_x, width_y), jnp.float32)
-    kappa_ext = extended[0, width : width + depth_planes]
-    global_plane = first + jnp.arange(depth_planes, dtype=jnp.int32)
-    at_receivers = (global_plane == 2).astype(jnp.float32)[:, None, None]
-    current = adj_now[0]
-    older = adj_prev[0]
-    for step in range(steps):
-        moment = steps - 1 - step
-        rimmed_field = with_halo(current[None], (("depth", 1),), 1)[0]
-        plane = source_plane(rows_x, rows_y, residual[0, moment], width_x, width_y)
-        spread = operate(rimmed_field, buoy_ext)[1:-1]
-        newer = (
-            2.0 * current - older + 0.08 * kappa_ext * spread + 0.08 * at_receivers * plane[None]
-        )
-        image = image + snaps[moment].astype(jnp.float32) * newer
-        older = current
-        current = newer
-    weighted = shot_count[0].astype(jnp.float32) * image
+    mat_ext = with_halo(packed, (("depth", 1),), HALO)
+    adj_ext = with_halo(jnp.stack([adj_now[0], adj_prev[0]]), (("depth", 1),), HALO)
+    holds_source = (lax.axis_index("depth") == 0).astype(jnp.float32)
+    src = jnp.stack(
+        [source_plane(rec_x[0], rec_y[0], residual[0, t], width_x, width_y) for t in range(steps)]
+    ) * holds_source
+    count = shot_count.astype(jnp.float32)
+    current, older, weighted = run_steps(count, adj_ext, mat_ext, fwd_snap[0], src)
     summed = scatter_rows(weighted, "shots", 1)
     grad_vel = 2.0 * density * velocity * summed / (4.0 * groups)
     return (current[None], older[None], grad_vel)

time: 200 us -> 130 us (0.65)
  the two profiles are of different devices: /device:TPU:24 before, /device:TPU:6 now
where the time goes in v2:
time: 130 us; the launch traced here: 129 us
  waiting for transfers between devices  62.1 us (48%)
  starting transfers between devices  34 us (26%)
  Pallas kernels  17.2 us (13%)
  other arithmetic  8.17 us (6%)
  local copies, waits for them, and re-layouts  4.64 us (4%)
  between operations  1.67 us (1%)
  matrix products  1.61 us (1%)
    ppermute x5, waiting for transfers between devices, gather_rows(): got = lax.ppermute(pieces, axis, pairs)  26 us
    ppermute x5, waiting for transfers between devices, scatter_rows(): got = lax.ppermute(send, axis, pairs)  24.1 us
    pallas_call x1, Pallas kernels, run_steps(): pl.pallas_call(stencil_kernel, out_shape=out_shape, in_specs=[pl.BlockSpe...  17.2 us
    ppermute x2, starting transfers between devices, with_halo(): before = lax.ppermute(last, axis, up)  12.5 us
    ppermute x5, starting transfers between devices, gather_rows(): got = lax.ppermute(pieces, axis, pairs)  12.1 us
    ppermute x2, waiting for transfers between devices, with_halo(): after = lax.ppermute(first, axis, down)  10.2 us
    ppermute x5, starting transfers between devices, scatter_rows(): got = lax.ppermute(send, axis, pairs)  5.53 us
    concatenate x2, other arithmetic, with_halo(): shard = jnp.concatenate([before, shard, after], axis=dim)  5.1 us
  transfers between devices with their start and end apart: 14, of which 12 were waited for; matrix products, arithmetic and copies ran while one was open for 6% of the time, Pallas kernels for 0%

profile of v2, /device:TPU:6, one launch (start us, length us, event | category | flops | bytes accessed | tf_op | source)
XLA Modules:
  0.0 129.4 jit_solution(17731326789966933946)
XLA Ops:
  0.6 0.8 fusion.20
  1.4 7.3 %collective-permute-start.2 = (f32[2,16,1,4,128]{4,1,3,0,2:T(8,128)S(1)}, f32[2,16,1,4,128]{4,1,3,0,2:T(8,128)S(1)}, u32[]{:S(2)}, u32[]{:S(2)}) collective-permute-start(f32[2,16,1,4,128]{4,1,3,0,2:T(8,128)S(1)} %maximum_bitcast_fusion.1), channel_id=1, source_target_pairs={{0,16},{1,17},{2,18},{3,19},{4,20},{5,21},{6,22},{7,23},{8,24},{9,... | collective-permute-start | bytes 196616 | tf_op jit(solution)/shard_map/ppermute | solution.py:137
  8.7 2.4 %collective-permute-done.2 = f32[2,16,1,4,128]{4,1,3,0,2:T(8,128)S(1)} collective-permute-done((f32[2,16,1,4,128]{4,1,3,0,2:T(8,128)S(1)}, f32[2,16,1,4,128]{4,1,3,0,2:T(8,128)S(1)}, u32[]{:S(2)}, u32[]{:S(2)}) %collective-permute-start.2) | collective-permute-done | bytes 65568 | tf_op jit(solution)/shard_map/ppermute | solution.py:137
  11.2 3.0 %collective-permute-start.3 = (f32[2,16,2,4,128]{4,1,3,2,0:T(8,128)S(1)}, f32[2,16,2,4,128]{4,1,3,2,0:T(8,128)S(1)}, u32[]{:S(2)}, u32[]{:S(2)}) collective-permute-start(f32[2,16,2,4,128]{4,1,3,2,0:T(8,128)S(1)} %maximum_bitcast_fusion), channel_id=1, source_target_pairs={{0,8},{1,9},{2,10},{3,11},{4,12},{5,13},{6,14},{7,15},{8,0},{9,1},... | collective-permute-start | bytes 393224 | tf_op jit(solution)/shard_map/ppermute | solution.py:137
  14.2 5.1 %collective-permute-done.3 = f32[2,16,2,4,128]{4,1,3,2,0:T(8,128)S(1)} collective-permute-done((f32[2,16,2,4,128]{4,1,3,2,0:T(8,128)S(1)}, f32[2,16,2,4,128]{4,1,3,2,0:T(8,128)S(1)}, u32[]{:S(2)}, u32[]{:S(2)}) %collective-permute-start.3) | collective-permute-done | bytes 131104 | tf_op jit(solution)/shard_map/ppermute | solution.py:137
  19.3 0.1 collective-permute-start.4
  19.4 7.6 %collective-permute-done.4 = f32[2,16,4,4,128]{4,1,3,2,0:T(8,128)S(1)} collective-permute-done((f32[2,16,4,4,128]{4,1,3,2,0:T(8,128)S(1)}, f32[2,16,4,4,128]{4,1,3,2,0:T(8,128)S(1)}, u32[]{:S(2)}, u32[]{:S(2)}) %collective-permute-start.4) | collective-permute-done | bytes 262176 | tf_op jit(solution)/shard_map/ppermute | solution.py:137
  27.2 1.7 %collective-permute-start.5 = (f32[2,16,8,4,128]{4,1,3,2,0:T(8,128)S(1)}, f32[2,16,8,4,128]{4,1,3,2,0:T(8,128)S(1)}, u32[]{:S(2)}, u32[]{:S(2)}) collective-permute-start(f32[2,16,8,4,128]{4,1,3,2,0:T(8,128)S(1)} %bitcast.93), channel_id=1, source_target_pairs={{0,2},{1,3},{2,0},{3,1},{4,6},{5,7},{6,4},{7,5},{8,10},{9,11},{10,... | collective-permute-start | bytes 1572872 | tf_op jit(solution)/shard_map/ppermute | solution.py:137
  28.8 10.8 %collective-permute-done.5 = f32[2,16,8,4,128]{4,1,3,2,0:T(8,128)S(1)} collective-permute-done((f32[2,16,8,4,128]{4,1,3,2,0:T(8,128)S(1)}, f32[2,16,8,4,128]{4,1,3,2,0:T(8,128)S(1)}, u32[]{:S(2)}, u32[]{:S(2)}) %collective-permute-start.5) | collective-permute-done | bytes 524320 | tf_op jit(solution)/shard_map/ppermute | solution.py:137
  39.6 0.1 select_bitcast_fusion.3
  39.7 0.0 copy-start.1
  39.8 0.1 pad_maximum_fusion.3
  39.9 0.0 copy-start.2
  39.9 0.1 copy.42
  40.0 0.1 collective-permute-start.6
  40.1 0.9 copy-done.1
  41.0 0.1 constant_dynamic-update-slice_fusion.1
  41.0 0.3 copy-done.2
  41.3 0.0 copy-start.5
  41.3 0.0 copy-start.6
  41.3 0.1 constant_dynamic-update-slice_fusion
  41.4 1.0 fusion.28
  42.4 5.0 %collective-permute-start = (f32[2,4,128,128]{3,2,1,0:T(8,128)}, f32[2,4,128,128]{3,2,1,0:T(8,128)}, u32[]{:S(2)}, u32[]{:S(2)}) collective-permute-start(f32[2,4,128,128]{3,2,1,0:T(8,128)} %get-tuple-element.16), channel_id=1, source_target_pairs={{0,32},{32,64},{64,96},{96,128},{128,160},{160,192},{192,224},{1,3... | collective-permute-start | bytes 1572872 | tf_op jit(solution)/shard_map/ppermute | solution.py:121
  47.5 1.9 %collective-permute-start.1 = (f32[2,4,128,128]{3,2,1,0:T(8,128)}, f32[2,4,128,128]{3,2,1,0:T(8,128)}, u32[]{:S(2)}, u32[]{:S(2)}) collective-permute-start(f32[2,4,128,128]{3,2,1,0:T(8,128)} %get-tuple-element.17), channel_id=1, source_target_pairs={{32,0},{64,32},{96,64},{128,96},{160,128},{192,160},{224,192},{33,... | collective-permute-start | bytes 1572872 | tf_op jit(solution)/shard_map/ppermute | solution.py:122
  50.0 0.0 copy-done.5
  50.1 0.0 copy-done.6
  50.1 0.0 copy-done.7
  50.1 0.4 convolution_bitcast_fusion
  50.5 0.4 convolution_bitcast_fusion.1
  50.9 0.0 collective-permute-done.6
  50.9 1.4 %select_bitcast_fusion.1 = (f32[2,16,16,1,4,128]{5,1,4,2,0,3:T(8,128)S(1)}, f32[2,16,16,1,4,128]{5,1,4,2,0,3:T(8,128)S(1)}) fusion(f32[2,16,16,4,128]{4,1,3,2,0:T(8,128)S(1)} %bitcast.92, f32[2,16,16,4,128]{4,1,3,2,0:T(8,128)} %collective-permute-done.6, pred[]{:T(512)S(6)} %eq.28), kind=kLoop, calls=%fused_computation.9 | loop fusion | flops 524288 | bytes 4194305 | tf_op jit(solution)/shard_map/stack | solution.py:141
  52.3 0.1 pad_maximum_fusion.2
  52.5 0.8 copy.43
  53.3 0.1 fusion.27
  53.4 7.5 %collective-permute-start.7 = (f32[2,4,128,128]{3,2,1,0:T(8,128)S(1)}, f32[2,4,128,128]{3,2,1,0:T(8,128)S(1)}, u32[]{:S(2)}, u32[]{:S(2)}) collective-permute-start(f32[2,4,128,128]{3,2,1,0:T(8,128)S(1)} %get-tuple-element.12), channel_id=1, source_target_pairs={{0,32},{32,64},{64,96},{96,128},{128,160},{160,192},{192,224},{1,3... | collective-permute-start | bytes 1572872 | tf_op jit(solution)/shard_map/ppermute | solution.py:121
  60.9 1.9 %collective-permute-start.8 = (f32[2,4,128,128]{3,2,1,0:T(8,128)S(1)}, f32[2,4,128,128]{3,2,1,0:T(8,128)S(1)}, u32[]{:S(2)}, u32[]{:S(2)}) collective-permute-start(f32[2,4,128,128]{3,2,1,0:T(8,128)S(1)} %get-tuple-element.13), channel_id=1, source_target_pairs={{32,0},{64,32},{96,64},{128,96},{160,128},{192,160},{224,192},{33,... | collective-permute-start | bytes 1572872 | tf_op jit(solution)/shard_map/ppermute | solution.py:122
  62.9 0.4 convolution_bitcast_fusion.2
  63.3 0.4 convolution_bitcast_fusion.3
  63.7 0.0 collective-permute-done
  63.7 2.5 %collective-permute-done.1 = f32[2,4,128,128]{3,2,1,0:T(8,128)} collective-permute-done((f32[2,4,128,128]{3,2,1,0:T(8,128)}, f32[2,4,128,128]{3,2,1,0:T(8,128)}, u32[]{:S(2)}, u32[]{:S(2)}) %collective-permute-start.1) | collective-permute-done | bytes 524320 | tf_op jit(solution)/shard_map/ppermute | solution.py:122
  66.2 3.1 %pad_maximum_fusion.adj_ref = f32[2,24,128,128]{3,2,1,0:T(8,128)} fusion(f32[2,4,128,128]{3,2,1,0:T(8,128)} %collective-permute-done.1, f32[2,16,128,128]{3,2,1,0:T(8,128)S(1)} %constant_dynamic-update-slice_fusion, f32[2,4,128,128]{3,2,1,0:T(8,128)} %collective-permute-done), kind=kLoop, calls=%fused_computation | loop fusion | flops 1572864 | bytes 6291456 | tf_op jit(solution)/shard_map/concatenate | solution.py:123
  69.3 1.8 %collective-permute-done.7 = f32[2,4,128,128]{3,2,1,0:T(8,128)S(1)} collective-permute-done((f32[2,4,128,128]{3,2,1,0:T(8,128)S(1)}, f32[2,4,128,128]{3,2,1,0:T(8,128)S(1)}, u32[]{:S(2)}, u32[]{:S(2)}) %collective-permute-start.7) | collective-permute-done | bytes 524320 | tf_op jit(solution)/shard_map/ppermute | solution.py:121
  71.1 7.7 %collective-permute-done.8 = f32[2,4,128,128]{3,2,1,0:T(8,128)S(1)} collective-permute-done((f32[2,4,128,128]{3,2,1,0:T(8,128)S(1)}, f32[2,4,128,128]{3,2,1,0:T(8,128)S(1)}, u32[]{:S(2)}, u32[]{:S(2)}) %collective-permute-start.8) | collective-permute-done | bytes 524320 | tf_op jit(solution)/shard_map/ppermute | solution.py:122
  78.8 2.0 %pad_maximum_fusion.1.mat_ref = f32[2,24,128,128]{3,2,1,0:T(8,128)} fusion(f32[2,4,128,128]{3,2,1,0:T(8,128)S(1)} %collective-permute-done.8, f32[2,16,128,128]{3,2,1,0:T(8,128)S(1)} %bitcast.90, f32[2,4,128,128]{3,2,1,0:T(8,128)S(1)} %collective-permute-done.7), kind=kLoop, calls=%fused_computation.1 | loop fusion | flops 1572864 | bytes 6291456 | tf_op jit(solution)/shard_map/concatenate | solution.py:123
  80.8 0.0 copy-done
  80.8 17.2 %shard_map.112 = (f32[16,128,128]{2,1,0:T(8,128)}, f32[16,128,128]{2,1,0:T(8,128)}, f32[16,128,128]{2,1,0:T(8,128)S(1)}) custom-call(f32[1]{0:T(128)S(6)} %convert_element_type.4.count_ref, f32[2,24,128,128]{3,2,1,0:T(8,128)} %pad_maximum_fusion.adj_ref, f32[2,24,128,128]{3,2,1,0:T(8,128)} %pad_maximum_fusion.1.mat_ref, ...), custom_call_target="tpu_custom_call" | custom-call | tf_op jit(solution)/shard_map/pallas_call | solution.py:103
  98.0 0.2 constant_dynamic-slice_fusion.1
  98.2 0.3 copy.56
  98.6 0.0 copy-start.3
  98.6 0.0 copy-start.4
  98.6 0.1 collective-permute-start.9
  98.7 1.9 %collective-permute-done.9 = f32[16,2,2,2,2,4,128]{6,0,5,4,3,2,1:T(8,128)S(1)} collective-permute-done((f32[16,2,2,2,2,4,128]{6,0,5,4,3,2,1:T(8,128)S(1)}, f32[16,2,2,2,2,4,128]{6,0,5,4,3,2,1:T(8,128)S(1)}, u32[]{:S(2)}, u32[]{:S(2)}) %collective-permute-start.9) | collective-permute-done | bytes 524320 | tf_op jit(solution)/shard_map/ppermute | solution.py:163
  100.6 0.3 bitcast_add_fusion
  100.9 0.8 collective-permute-start.10
  101.7 7.7 %collective-permute-done.10 = f32[16,2,2,2,4,128]{5,0,4,3,2,1:T(8,128)S(1)} collective-permute-done((f32[16,2,2,2,4,128]{5,0,4,3,2,1:T(8,128)S(1)}, f32[16,2,2,2,4,128]{5,0,4,3,2,1:T(8,128)S(1)}, u32[]{:S(2)}, u32[]{:S(2)}) %collective-permute-start.10) | collective-permute-done | bytes 262176 | tf_op jit(solution)/shard_map/ppermute | solution.py:163
  109.4 0.7 collective-permute-start.11
  110.1 4.4 %collective-permute-done.11 = f32[16,2,2,4,128]{4,0,3,2,1:T(8,128)S(1)} collective-permute-done((f32[16,2,2,4,128]{4,0,3,2,1:T(8,128)S(1)}, f32[16,2,2,4,128]{4,0,3,2,1:T(8,128)S(1)}, u32[]{:S(2)}, u32[]{:S(2)}) %collective-permute-start.11) | collective-permute-done | bytes 131104 | tf_op jit(solution)/shard_map/ppermute | solution.py:163
  114.5 0.1 collective-permute-start.12
  114.6 5.9 %collective-permute-done.12 = f32[16,2,4,128]{3,0,2,1:T(8,128)S(1)} collective-permute-done((f32[16,2,4,128]{3,0,2,1:T(8,128)S(1)}, f32[16,2,4,128]{3,0,2,1:T(8,128)S(1)}, u32[]{:S(2)}, u32[]{:S(2)}) %collective-permute-start.12) | collective-permute-done | bytes 65568 | tf_op jit(solution)/shard_map/ppermute | solution.py:163
  120.5 3.9 %collective-permute-start.13 = (f32[16,4,128]{2,0,1:T(8,128)S(1)}, f32[16,4,128]{2,0,1:T(8,128)S(1)}, u32[]{:S(2)}, u32[]{:S(2)}) collective-permute-start(f32[16,4,128]{2,0,1:T(8,128)S(1)} %dynamic-slice_bitcast_fusion.3), channel_id=1, source_target_pairs={{0,16},{1,17},{2,18},{3,19},{4,20},{5,21},{6,22},{7,23},{8,24},{9,... | collective-permute-start | bytes 98312 | tf_op jit(solution)/shard_map/ppermute | solution.py:163
  124.4 4.3 %collective-permute-done.13 = f32[16,4,128]{2,0,1:T(8,128)S(1)} collective-permute-done((f32[16,4,128]{2,0,1:T(8,128)S(1)}, f32[16,4,128]{2,0,1:T(8,128)S(1)}, u32[]{:S(2)}, u32[]{:S(2)}) %collective-permute-start.13) | collective-permute-done | bytes 32800 | tf_op jit(solution)/shard_map/ppermute | solution.py:163
  128.7 0.0 copy-done.3
  128.7 0.0 copy-done.4
  128.7 0.6 copy.48
  (20 shorter events, 0.4 us)
Async XLA Ops:
  1.4 9.7 %collective-permute-start.2 = (f32[2,16,1,4,128]{4,1,3,0,2:T(8,128)S(1)}, f32[2,16,1,4,128]{4,1,3,0,2:T(8,128)S(1)}, u32[]{:S(2)}, u32[]{:S(2)}) collective-permute-start(f32[2,16,1,4,128]{4,1,3,0,2:T(8,128)S(1)} %maximum_bitcast_fusion.1), channel_id=1, source_target_pairs={{0,16},{1,17},{2,18},{3,19},{4,20},{5,21},{6,22},{7,23},{8,24},{9,... | collective-permute-start | bytes 196616 | tf_op jit(solution)/shard_map/ppermute | solution.py:137
  11.2 8.1 %collective-permute-start.3 = (f32[2,16,2,4,128]{4,1,3,2,0:T(8,128)S(1)}, f32[2,16,2,4,128]{4,1,3,2,0:T(8,128)S(1)}, u32[]{:S(2)}, u32[]{:S(2)}) collective-permute-start(f32[2,16,2,4,128]{4,1,3,2,0:T(8,128)S(1)} %maximum_bitcast_fusion), channel_id=1, source_target_pairs={{0,8},{1,9},{2,10},{3,11},{4,12},{5,13},{6,14},{7,15},{8,0},{9,1},... | collective-permute-start | bytes 393224 | tf_op jit(solution)/shard_map/ppermute | solution.py:137
  19.3 7.7 %collective-permute-start.4 = (f32[2,16,4,4,128]{4,1,3,2,0:T(8,128)S(1)}, f32[2,16,4,4,128]{4,1,3,2,0:T(8,128)S(1)}, u32[]{:S(2)}, u32[]{:S(2)}) collective-permute-start(f32[2,16,4,4,128]{4,1,3,2,0:T(8,128)S(1)} %bitcast.95), channel_id=1, source_target_pairs={{0,4},{1,5},{2,6},{3,7},{4,0},{5,1},{6,2},{7,3},{8,12},{9,13},{10,... | collective-permute-start | bytes 786440 | tf_op jit(solution)/shard_map/ppermute | solution.py:137
  27.2 12.5 %collective-permute-start.5 = (f32[2,16,8,4,128]{4,1,3,2,0:T(8,128)S(1)}, f32[2,16,8,4,128]{4,1,3,2,0:T(8,128)S(1)}, u32[]{:S(2)}, u32[]{:S(2)}) collective-permute-start(f32[2,16,8,4,128]{4,1,3,2,0:T(8,128)S(1)} %bitcast.93), channel_id=1, source_target_pairs={{0,2},{1,3},{2,0},{3,1},{4,6},{5,7},{6,4},{7,5},{8,10},{9,11},{10,... | collective-permute-start | bytes 1572872 | tf_op jit(solution)/shard_map/ppermute | solution.py:137
  39.7 1.2 copy-start.1
  39.9 1.5 %copy-start.2 = (f32[1,16,128,128]{3,2,1,0:T(8,128)S(1)}, f32[1,16,128,128]{3,2,1,0:T(8,128)}, u32[]{:S(2)}) copy-start(f32[1,16,128,128]{3,2,1,0:T(8,128)} %param.10) | copy-start | bytes 3145732
  40.0 11.0 %collective-permute-start.6 = (f32[2,16,16,4,128]{4,1,3,2,0:T(8,128)S(1)}, f32[2,16,16,4,128]{4,1,3,2,0:T(8,128)}, u32[]{:S(2)}, u32[]{:S(2)}) collective-permute-start(f32[2,16,16,4,128]{4,1,3,2,0:T(8,128)S(1)} %bitcast.91), channel_id=1, source_target_pairs={{0,1},{1,0},{2,3},{3,2},{4,5},{5,4},{6,7},{7,6},{8,9},{9,8},{10,11... | collective-permute-start | bytes 3145736 | tf_op jit(solution)/shard_map/ppermute | solution.py:137
  41.3 8.7 %copy-start.5 = (f32[1,4,256]{2,1,0:T(4,128)S(1)}, f32[1,4,256]{2,1,0:T(4,128)}, u32[]{:S(2)}) copy-start(f32[1,4,256]{2,1,0:T(4,128)} %param.17) | copy-start | bytes 12292
  41.3 8.8 %copy-start.6 = (s32[1,256]{1,0:T(1,128)S(1)}, s32[1,256]{1,0:T(1,128)}, u32[]{:S(2)}) copy-start(s32[1,256]{1,0:T(1,128)} %param.16) | copy-start | bytes 3076
  41.3 8.8 %copy-start.7 = (s32[1,256]{1,0:T(1,128)S(1)}, s32[1,256]{1,0:T(1,128)}, u32[]{:S(2)}) copy-start(s32[1,256]{1,0:T(1,128)} %param.15) | copy-start | bytes 3076
  42.4 21.3 %collective-permute-start = (f32[2,4,128,128]{3,2,1,0:T(8,128)}, f32[2,4,128,128]{3,2,1,0:T(8,128)}, u32[]{:S(2)}, u32[]{:S(2)}) collective-permute-start(f32[2,4,128,128]{3,2,1,0:T(8,128)} %get-tuple-element.16), channel_id=1, source_target_pairs={{0,32},{32,64},{64,96},{96,128},{128,160},{160,192},{192,224},{1,3... | collective-permute-start | bytes 1572872 | tf_op jit(solution)/shard_map/ppermute | solution.py:121
  47.5 18.7 %collective-permute-start.1 = (f32[2,4,128,128]{3,2,1,0:T(8,128)}, f32[2,4,128,128]{3,2,1,0:T(8,128)}, u32[]{:S(2)}, u32[]{:S(2)}) collective-permute-start(f32[2,4,128,128]{3,2,1,0:T(8,128)} %get-tuple-element.17), channel_id=1, source_target_pairs={{32,0},{64,32},{96,64},{128,96},{160,128},{192,160},{224,192},{33,... | collective-permute-start | bytes 1572872 | tf_op jit(solution)/shard_map/ppermute | solution.py:122
  53.4 17.7 %collective-permute-start.7 = (f32[2,4,128,128]{3,2,1,0:T(8,128)S(1)}, f32[2,4,128,128]{3,2,1,0:T(8,128)S(1)}, u32[]{:S(2)}, u32[]{:S(2)}) collective-permute-start(f32[2,4,128,128]{3,2,1,0:T(8,128)S(1)} %get-tuple-element.12), channel_id=1, source_target_pairs={{0,32},{32,64},{64,96},{96,128},{128,160},{160,192},{192,224},{1,3... | collective-permute-start | bytes 1572872 | tf_op jit(solution)/shard_map/ppermute | solution.py:121
  60.9 17.9 %collective-permute-start.8 = (f32[2,4,128,128]{3,2,1,0:T(8,128)S(1)}, f32[2,4,128,128]{3,2,1,0:T(8,128)S(1)}, u32[]{:S(2)}, u32[]{:S(2)}) collective-permute-start(f32[2,4,128,128]{3,2,1,0:T(8,128)S(1)} %get-tuple-element.13), channel_id=1, source_target_pairs={{32,0},{64,32},{96,64},{128,96},{160,128},{192,160},{224,192},{33,... | collective-permute-start | bytes 1572872 | tf_op jit(solution)/shard_map/ppermute | solution.py:122
  69.3 11.6 %copy-start = (bf16[1,4,16,128,128]{4,3,2,1,0:T(8,128)(2,1)S(1)}, bf16[1,4,16,128,128]{4,3,2,1,0:T(8,128)(2,1)}, u32[]{:S(2)}) copy-start(bf16[1,4,16,128,128]{4,3,2,1,0:T(8,128)(2,1)} %param.11) | copy-start | bytes 6291460
  98.6 30.2 %copy-start.3 = (f32[16,4,128]{2,1,0:T(4,128)S(1)}, f32[16,4,128]{2,1,0:T(4,128)}, u32[]{:S(2)}) copy-start(f32[16,4,128]{2,1,0:T(4,128)} %param.12) | copy-start | bytes 98308
  98.6 30.2 %copy-start.4 = (f32[16,4,128]{2,1,0:T(4,128)S(1)}, f32[16,4,128]{2,1,0:T(4,128)}, u32[]{:S(2)}) copy-start(f32[16,4,128]{2,1,0:T(4,128)} %param.13) | copy-start | bytes 98308
  98.6 2.0 %collective-permute-start.9 = (f32[16,2,2,2,2,4,128]{6,0,5,4,3,2,1:T(8,128)S(1)}, f32[16,2,2,2,2,4,128]{6,0,5,4,3,2,1:T(8,128)S(1)}, u32[]{:S(2)}, u32[]{:S(2)}) collective-permute-start(f32[16,2,2,2,2,4,128]{6,0,5,4,3,2,1:T(8,128)S(1)} %bitcast.97), channel_id=1, source_target_pairs={{0,1},{1,0},{2,3},{3,2},{4,5},{5,4},{6,7},{7,6},{8,9},{9,8},{10,11... | collective-permute-start | bytes 1572872 | tf_op jit(solution)/shard_map/ppermute | solution.py:163
  100.9 8.4 %collective-permute-start.10 = (f32[16,2,2,2,4,128]{5,0,4,3,2,1:T(8,128)S(1)}, f32[16,2,2,2,4,128]{5,0,4,3,2,1:T(8,128)S(1)}, u32[]{:S(2)}, u32[]{:S(2)}) collective-permute-start(f32[16,2,2,2,4,128]{5,0,4,3,2,1:T(8,128)S(1)} %dynamic-slice_bitcast_fusion), channel_id=1, source_target_pairs={{0,2},{1,3},{2,0},{3,1},{4,6},{5,7},{6,4},{7,5},{8,10},{9,11},{10,... | collective-permute-start | bytes 786440 | tf_op jit(solution)/shard_map/ppermute | solution.py:163
  109.4 5.1 %collective-permute-start.11 = (f32[16,2,2,4,128]{4,0,3,2,1:T(8,128)S(1)}, f32[16,2,2,4,128]{4,0,3,2,1:T(8,128)S(1)}, u32[]{:S(2)}, u32[]{:S(2)}) collective-permute-start(f32[16,2,2,4,128]{4,0,3,2,1:T(8,128)S(1)} %dynamic-slice_bitcast_fusion.1), channel_id=1, source_target_pairs={{0,4},{1,5},{2,6},{3,7},{4,0},{5,1},{6,2},{7,3},{8,12},{9,13},{10,... | collective-permute-start | bytes 393224 | tf_op jit(solution)/shard_map/ppermute | solution.py:163
  114.5 6.0 %collective-permute-start.12 = (f32[16,2,4,128]{3,0,2,1:T(8,128)S(1)}, f32[16,2,4,128]{3,0,2,1:T(8,128)S(1)}, u32[]{:S(2)}, u32[]{:S(2)}) collective-permute-start(f32[16,2,4,128]{3,0,2,1:T(8,128)S(1)} %dynamic-slice_bitcast_fusion.2), channel_id=1, source_target_pairs={{0,8},{1,9},{2,10},{3,11},{4,12},{5,13},{6,14},{7,15},{8,0},{9,1},... | collective-permute-start | bytes 196616 | tf_op jit(solution)/shard_map/ppermute | solution.py:163
  120.5 8.2 %collective-permute-start.13 = (f32[16,4,128]{2,0,1:T(8,128)S(1)}, f32[16,4,128]{2,0,1:T(8,128)S(1)}, u32[]{:S(2)}, u32[]{:S(2)}) collective-permute-start(f32[16,4,128]{2,0,1:T(8,128)S(1)} %dynamic-slice_bitcast_fusion.3), channel_id=1, source_target_pairs={{0,16},{1,17},{2,18},{3,19},{4,20},{5,21},{6,22},{7,23},{8,24},{9,... | collective-permute-start | bytes 98312 | tf_op jit(solution)/shard_map/ppermute | solution.py:163
